TPU v7x, 256 devices: a whole 4x4x8 slice. The times are simulated.
256 devices in a mesh: req: 64 (over y, z_lo, x, core), tp: 4 (over z_hi).
Axes of the slice: x: 4, y: 4, z: 8 (z_hi: 4, z_lo: 2; z = z_hi * 2 + z_lo), core: 2. Of those that a mesh axis runs over, the one named last changes fastest.
Arguments:
- tokens: bfloat16 [16384, 2048], P('req'), may hold values from -6 to 6
- norm_gain: float32 [2048], replicated, may hold values from 0.25 to 1.75
- w_query: bfloat16 [2048, 2048], P(None, 'tp'), may hold values from -1 to 1
- w_key: bfloat16 [2048, 2048], P(None, 'tp'), may hold values from -1 to 1
- w_value: bfloat16 [2048, 2048], P(None, 'tp'), may hold values from -0.125 to 0.125
- w_out: bfloat16 [2048, 2048], P('tp'), may hold values from -0.125 to 0.125
- lambdas: float32 [4, 8, 128], P(None, 'tp'), may hold values from -1 to 1
- sub_gain: float32 [8, 256], P('tp'), may hold values from 0.5 to 2
- lengths: int32 [4], replicated, may hold values from 1 to 8192, 16384 in all
Outputs:
- hidden: bfloat16 [16384, 2048], P('req')
- key_cache: bfloat16 [16384, 2048], P('req', 'tp')
- value_cache: bfloat16 [16384, 2048], P('req', 'tp')
Inputs may be any that keep to these rules, and one draw needn't show every extreme that they name: The lengths sum to 16384; the longest is exactly 8192.
All inputs are finite; a program needn't handle non-finite values.
Results may differ from a plain program's by a relative error of at most 0.007.
Values may be sent and summed in bfloat16 or wider, within the bound.
No kernel may reach another device: no remote copies, remote signals or barrier semaphores. Data moves between devices by JAX's collectives and lax.ppermute only.
A program may use at most 128 MiB of HBM per device.

v0:
```python
import math

import jax
import jax.numpy as jnp
from jax import lax
from jax.sharding import PartitionSpec as P

QK = 128
VD = 256


lambda_start = 0.8 - 0.6 * math.exp(-3.3)
masked_score = -1e30


def shifted(value, axis, steps):
    count = lax.axis_size(axis)
    first, last = (max(0, -steps), min(count, count - steps))
    return lax.ppermute(value, axis, [(source, source + steps) for source in range(first, last)])


def locate(index, lengths):
    ends = jnp.cumsum(lengths)
    starts = ends - lengths
    segment = jnp.sum((ends[None, :] <= index[:, None]).astype(jnp.int32), axis=1)
    hit = jnp.arange(lengths.shape[0], dtype=jnp.int32)[None, :] == segment[:, None]
    begin = jnp.sum(jnp.where(hit, starts[None, :], 0), axis=1)
    return (segment, index - begin)


def rotate(proj, position):
    half = proj.shape[-1] // 2
    freq = 10000.0 ** (-jnp.arange(half, dtype=jnp.float32) / half)
    angle = position.astype(jnp.float32)[:, None] * freq[None, :]
    cosine = jnp.cos(angle)[:, None, None, :]
    sine = jnp.sin(angle)[:, None, None, :]
    front = proj[..., :half]
    back = proj[..., half:]
    return jnp.concatenate([front * cosine - back * sine, back * cosine + front * sine], axis=-1)


def on_device(tokens, norm_gain, w_query, w_key, w_value, w_out, lambdas, sub_gain, lengths):
    rows = tokens.shape[0]
    heads = w_query.shape[1] // (2 * QK)
    key_cols = heads * 2 * QK
    total = rows * lax.axis_size("req")
    longest = min(8192, total // 2)
    reach = longest // rows
    first = lax.axis_index("req") * rows
    local_index = first + jnp.arange(rows, dtype=jnp.int32)
    seg_query, pos_query = locate(local_index, lengths)
    xf = tokens.astype(jnp.float32)
    normed = (xf * lax.rsqrt(jnp.mean(xf * xf, axis=-1, keepdims=True) + 1e-06) * norm_gain).astype(
        jnp.bfloat16
    )
    query = rotate(
        jnp.dot(normed, w_query, preferred_element_type=jnp.float32).reshape(rows, heads, 2, QK),
        pos_query,
    ).astype(jnp.bfloat16)
    keys = rotate(
        jnp.dot(normed, w_key, preferred_element_type=jnp.float32).reshape(rows, heads, 2, QK),
        pos_query,
    ).astype(jnp.bfloat16)
    values = jnp.dot(normed, w_value, preferred_element_type=jnp.float32).astype(jnp.bfloat16)
    key_flat = keys.reshape(rows, key_cols)
    own = jnp.concatenate([key_flat, values], axis=1)
    lam = (
        jnp.exp(jnp.sum(lambdas[0] * lambdas[1], axis=-1))
        - jnp.exp(jnp.sum(lambdas[2] * lambdas[3], axis=-1))
        + lambda_start
    )
    scale = QK ** (-0.5)

    def absorb(state, shard, anchor):
        key_index = anchor + jnp.arange(rows, dtype=jnp.int32)
        key_seg, unused = locate(key_index, lengths)
        allowed = (
            (key_index >= 0)[None, :]
            & (key_index[None, :] <= local_index[:, None])
            & (key_seg[None, :] == seg_query[:, None])
        )

        def compute(carry):
            top, mass, acc = carry
            shard_keys = shard[:, :key_cols].reshape(rows, heads, 2, QK)
            shard_values = shard[:, key_cols:].reshape(rows, heads, VD)
            scores = (
                jnp.einsum("qhmd,khmd->mhqk", query, shard_keys, preferred_element_type=jnp.float32)
                * scale
            )
            scores = jnp.where(allowed, scores, masked_score)
            new_top = jnp.maximum(top, jnp.max(scores, axis=-1))
            weights = jnp.where(allowed, jnp.exp(scores - new_top[..., None]), 0.0)
            fade = jnp.exp(top - new_top)
            mass = mass * fade + jnp.sum(weights, axis=-1)
            acc = acc * fade[..., None] + jnp.einsum(
                "mhqk,khv->mhqv",
                weights.astype(jnp.bfloat16),
                shard_values,
                preferred_element_type=jnp.float32,
            )
            return (new_top, mass, acc)

        def keep(carry):
            return carry

        return lax.cond(jnp.any(allowed), compute, keep, state)

    start = (
        jnp.full((2, heads, rows), masked_score, jnp.float32),
        jnp.zeros((2, heads, rows), jnp.float32),
        jnp.zeros((2, heads, rows, VD), jnp.float32),
    )
    state = absorb(start, own, first)

    def turn(step, carry):
        current, moving = carry
        moving = shifted(moving, "req", 1)
        return (absorb(current, moving, first - (step + 1) * rows), moving)

    state, unused = lax.fori_loop(0, reach, turn, (state, own))
    top, mass, acc = state
    attended = acc / mass[..., None]
    diff = attended[0] - lam[:, None, None] * attended[1]
    normed_heads = (
        diff
        * lax.rsqrt(jnp.mean(diff * diff, axis=-1, keepdims=True) + 1e-05)
        * sub_gain[:, None, :]
        * (1.0 - lambda_start)
    )
    merged = jnp.transpose(normed_heads, (1, 0, 2)).reshape(rows, heads * VD).astype(jnp.bfloat16)
    summed = lax.psum(
        jnp.dot(merged, w_out, preferred_element_type=jnp.float32).astype(jnp.bfloat16), "tp"
    ).astype(jnp.float32)
    hidden = (xf + summed).astype(jnp.bfloat16)
    return (hidden, key_flat, values)


def solution(mesh):
    in_specs = (
        P("req", None),
        P(),
        P(None, "tp"),
        P(None, "tp"),
        P(None, "tp"),
        P("tp", None),
        P(None, "tp", None),
        P("tp", None),
        P(),
    )
    out_specs = (P("req", None), P("req", "tp"), P("req", "tp"))
    return jax.shard_map(
        on_device, mesh=mesh, in_specs=in_specs, out_specs=out_specs, check_vma=False
    )
```

profile of v0, /device:TPU:1, one launch (start us, length us, event | category | flops | bytes accessed | tf_op | source)
XLA Modules:
  0.0 688.0 jit_solution(657436987407801427)
XLA Ops:
  34.9 410.5 %while.23 = (s32[]{:T(128)}, f32[2,2,256]{2,1,0:T(2,128)}, f32[2,2,256]{2,1,0:T(2,128)S(1)}, f32[2,2,256,256]{3,2,0,1:T(8,128)}, bf16[256,1024]{0,1:T(8,128)(2,1...) while((s32[]{:T(128)}, f32[2,2,256]{2,1,0:T(2,128)}, ...), condition=%wide.region_17.18_spmd.clone.clone, body=%wide.region_10.17_spmd.clone.clone.sunk | while | flops 204019456 | bytes 10498871 | solution.py:121
  40.9 4.9 collective-permute-done
  45.8 5.2 conditional.6
  57.6 4.9 collective-permute-done
  63.3 9.5 %collective-permute-start = (bf16[256,1024]{0,1:T(8,128)(2,1)}, bf16[256,1024]{0,1:T(8,128)(2,1)S(1)}, u32[]{:S(2)}, u32[]{:S(2)}) collective-permute-start(bf16[256,1024]{0,1:T(8,128)(2,1)} %get-tuple-element.507), channel_id=1, source_target_pairs={{0,4},{4,8},{8,12},{12,16},{16,20},{20,24},{24,28},{28,32},{32,36}... | collective-permute-start | bytes 1572872 | tf_op jit(solution)/shard_map/while/body/eval_jaxpr/ppermute | solution.py:19
  74.3 4.9 collective-permute-done
  85.8 4.9 collective-permute-done
  97.3 4.9 collective-permute-done
  108.8 4.9 collective-permute-done
  114.5 6.9 %collective-permute-start = (bf16[256,1024]{0,1:T(8,128)(2,1)}, bf16[256,1024]{0,1:T(8,128)(2,1)S(1)}, u32[]{:S(2)}, u32[]{:S(2)}) collective-permute-start(bf16[256,1024]{0,1:T(8,128)(2,1)} %get-tuple-element.507), channel_id=1, source_target_pairs={{0,4},{4,8},{8,12},{12,16},{16,20},{20,24},{24,28},{28,32},{32,36}... | collective-permute-start | bytes 1572872 | tf_op jit(solution)/shard_map/while/body/eval_jaxpr/ppermute | solution.py:19
  122.9 4.9 collective-permute-done
  134.4 4.9 collective-permute-done
  145.9 4.9 collective-permute-done
  157.4 4.9 collective-permute-done
  163.1 6.6 collective-permute-start
  171.2 4.9 collective-permute-done
  182.7 4.9 collective-permute-done
  194.2 4.9 collective-permute-done
  268.8 6.0 collective-permute-start
  282.1 6.4 collective-permute-start
  295.7 6.4 collective-permute-start
  309.3 6.4 collective-permute-start
  322.9 6.4 collective-permute-start
  336.5 6.4 collective-permute-start
  350.1 6.4 collective-permute-start
  363.7 6.4 collective-permute-start
  377.3 6.4 collective-permute-start
  390.9 6.4 collective-permute-start
  404.5 6.4 collective-permute-start
  418.1 6.4 collective-permute-start
  431.7 6.5 collective-permute-start
  449.6 228.9 %all-reduce.2.cloned.1.call-done = bf16[256,2048]{1,0:T(8,128)(2,1)} async-done(((bf16[256,2048]{1,0:T(8,128)(2,1)}), bf16[256,2048]{1,0:T(8,128)(2,1)}) %all-reduce.2.cloned.1.call-update) | async-done | bytes 1048592 | tf_op jit(solution)/shard_map/psum | solution.py:132
  (340 shorter events, 258.9 us)
Async XLA Ops:
  7.2 671.4 %all-reduce.2.cloned.1.call-start = ((), (), s32[]{:S(2)}) async-start(), calls=%async_computation | async-start | bytes 2097152 | tf_op jit(solution)/shard_map/psum | solution.py:132
  34.9 10.9 %collective-permute-start = (bf16[256,1024]{0,1:T(8,128)(2,1)}, bf16[256,1024]{0,1:T(8,128)(2,1)S(1)}, u32[]{:S(2)}, u32[]{:S(2)}) collective-permute-start(bf16[256,1024]{0,1:T(8,128)(2,1)} %get-tuple-element.507), channel_id=1, source_target_pairs={{0,4},{4,8},{8,12},{12,16},{16,20},{20,24},{24,28},{28,32},{32,36}... | collective-permute-start | bytes 1572872 | tf_op jit(solution)/shard_map/while/body/eval_jaxpr/ppermute | solution.py:19
  51.8 10.7 %collective-permute-start = (bf16[256,1024]{0,1:T(8,128)(2,1)}, bf16[256,1024]{0,1:T(8,128)(2,1)S(1)}, u32[]{:S(2)}, u32[]{:S(2)}) collective-permute-start(bf16[256,1024]{0,1:T(8,128)(2,1)} %get-tuple-element.507), channel_id=1, source_target_pairs={{0,4},{4,8},{8,12},{12,16},{16,20},{20,24},{24,28},{28,32},{32,36}... | collective-permute-start | bytes 1572872 | tf_op jit(solution)/shard_map/while/body/eval_jaxpr/ppermute | solution.py:19
  63.3 15.9 %collective-permute-start = (bf16[256,1024]{0,1:T(8,128)(2,1)}, bf16[256,1024]{0,1:T(8,128)(2,1)S(1)}, u32[]{:S(2)}, u32[]{:S(2)}) collective-permute-start(bf16[256,1024]{0,1:T(8,128)(2,1)} %get-tuple-element.507), channel_id=1, source_target_pairs={{0,4},{4,8},{8,12},{12,16},{16,20},{20,24},{24,28},{28,32},{32,36}... | collective-permute-start | bytes 1572872 | tf_op jit(solution)/shard_map/while/body/eval_jaxpr/ppermute | solution.py:19
  80.1 10.7 %collective-permute-start = (bf16[256,1024]{0,1:T(8,128)(2,1)}, bf16[256,1024]{0,1:T(8,128)(2,1)S(1)}, u32[]{:S(2)}, u32[]{:S(2)}) collective-permute-start(bf16[256,1024]{0,1:T(8,128)(2,1)} %get-tuple-element.507), channel_id=1, source_target_pairs={{0,4},{4,8},{8,12},{12,16},{16,20},{20,24},{24,28},{28,32},{32,36}... | collective-permute-start | bytes 1572872 | tf_op jit(solution)/shard_map/while/body/eval_jaxpr/ppermute | solution.py:19
  91.5 10.7 %collective-permute-start = (bf16[256,1024]{0,1:T(8,128)(2,1)}, bf16[256,1024]{0,1:T(8,128)(2,1)S(1)}, u32[]{:S(2)}, u32[]{:S(2)}) collective-permute-start(bf16[256,1024]{0,1:T(8,128)(2,1)} %get-tuple-element.507), channel_id=1, source_target_pairs={{0,4},{4,8},{8,12},{12,16},{16,20},{20,24},{24,28},{28,32},{32,36}... | collective-permute-start | bytes 1572872 | tf_op jit(solution)/shard_map/while/body/eval_jaxpr/ppermute | solution.py:19
  103.0 10.7 %collective-permute-start = (bf16[256,1024]{0,1:T(8,128)(2,1)}, bf16[256,1024]{0,1:T(8,128)(2,1)S(1)}, u32[]{:S(2)}, u32[]{:S(2)}) collective-permute-start(bf16[256,1024]{0,1:T(8,128)(2,1)} %get-tuple-element.507), channel_id=1, source_target_pairs={{0,4},{4,8},{8,12},{12,16},{16,20},{20,24},{24,28},{28,32},{32,36}... | collective-permute-start | bytes 1572872 | tf_op jit(solution)/shard_map/while/body/eval_jaxpr/ppermute | solution.py:19
  114.5 13.3 %collective-permute-start = (bf16[256,1024]{0,1:T(8,128)(2,1)}, bf16[256,1024]{0,1:T(8,128)(2,1)S(1)}, u32[]{:S(2)}, u32[]{:S(2)}) collective-permute-start(bf16[256,1024]{0,1:T(8,128)(2,1)} %get-tuple-element.507), channel_id=1, source_target_pairs={{0,4},{4,8},{8,12},{12,16},{16,20},{20,24},{24,28},{28,32},{32,36}... | collective-permute-start | bytes 1572872 | tf_op jit(solution)/shard_map/while/body/eval_jaxpr/ppermute | solution.py:19
  128.6 10.7 %collective-permute-start = (bf16[256,1024]{0,1:T(8,128)(2,1)}, bf16[256,1024]{0,1:T(8,128)(2,1)S(1)}, u32[]{:S(2)}, u32[]{:S(2)}) collective-permute-start(bf16[256,1024]{0,1:T(8,128)(2,1)} %get-tuple-element.507), channel_id=1, source_target_pairs={{0,4},{4,8},{8,12},{12,16},{16,20},{20,24},{24,28},{28,32},{32,36}... | collective-permute-start | bytes 1572872 | tf_op jit(solution)/shard_map/while/body/eval_jaxpr/ppermute | solution.py:19
  140.1 10.7 %collective-permute-start = (bf16[256,1024]{0,1:T(8,128)(2,1)}, bf16[256,1024]{0,1:T(8,128)(2,1)S(1)}, u32[]{:S(2)}, u32[]{:S(2)}) collective-permute-start(bf16[256,1024]{0,1:T(8,128)(2,1)} %get-tuple-element.507), channel_id=1, source_target_pairs={{0,4},{4,8},{8,12},{12,16},{16,20},{20,24},{24,28},{28,32},{32,36}... | collective-permute-start | bytes 1572872 | tf_op jit(solution)/shard_map/while/body/eval_jaxpr/ppermute | solution.py:19
  151.6 10.7 %collective-permute-start = (bf16[256,1024]{0,1:T(8,128)(2,1)}, bf16[256,1024]{0,1:T(8,128)(2,1)S(1)}, u32[]{:S(2)}, u32[]{:S(2)}) collective-permute-start(bf16[256,1024]{0,1:T(8,128)(2,1)} %get-tuple-element.507), channel_id=1, source_target_pairs={{0,4},{4,8},{8,12},{12,16},{16,20},{20,24},{24,28},{28,32},{32,36}... | collective-permute-start | bytes 1572872 | tf_op jit(solution)/shard_map/while/body/eval_jaxpr/ppermute | solution.py:19
  163.1 13.0 %collective-permute-start = (bf16[256,1024]{0,1:T(8,128)(2,1)}, bf16[256,1024]{0,1:T(8,128)(2,1)S(1)}, u32[]{:S(2)}, u32[]{:S(2)}) collective-permute-start(bf16[256,1024]{0,1:T(8,128)(2,1)} %get-tuple-element.507), channel_id=1, source_target_pairs={{0,4},{4,8},{8,12},{12,16},{16,20},{20,24},{24,28},{28,32},{32,36}... | collective-permute-start | bytes 1572872 | tf_op jit(solution)/shard_map/while/body/eval_jaxpr/ppermute | solution.py:19
  176.9 10.7 %collective-permute-start = (bf16[256,1024]{0,1:T(8,128)(2,1)}, bf16[256,1024]{0,1:T(8,128)(2,1)S(1)}, u32[]{:S(2)}, u32[]{:S(2)}) collective-permute-start(bf16[256,1024]{0,1:T(8,128)(2,1)} %get-tuple-element.507), channel_id=1, source_target_pairs={{0,4},{4,8},{8,12},{12,16},{16,20},{20,24},{24,28},{28,32},{32,36}... | collective-permute-start | bytes 1572872 | tf_op jit(solution)/shard_map/while/body/eval_jaxpr/ppermute | solution.py:19
  188.4 10.7 %collective-permute-start = (bf16[256,1024]{0,1:T(8,128)(2,1)}, bf16[256,1024]{0,1:T(8,128)(2,1)S(1)}, u32[]{:S(2)}, u32[]{:S(2)}) collective-permute-start(bf16[256,1024]{0,1:T(8,128)(2,1)} %get-tuple-element.507), channel_id=1, source_target_pairs={{0,4},{4,8},{8,12},{12,16},{16,20},{20,24},{24,28},{28,32},{32,36}... | collective-permute-start | bytes 1572872 | tf_op jit(solution)/shard_map/while/body/eval_jaxpr/ppermute | solution.py:19
  199.9 10.7 %collective-permute-start = (bf16[256,1024]{0,1:T(8,128)(2,1)}, bf16[256,1024]{0,1:T(8,128)(2,1)S(1)}, u32[]{:S(2)}, u32[]{:S(2)}) collective-permute-start(bf16[256,1024]{0,1:T(8,128)(2,1)} %get-tuple-element.507), channel_id=1, source_target_pairs={{0,4},{4,8},{8,12},{12,16},{16,20},{20,24},{24,28},{28,32},{32,36}... | collective-permute-start | bytes 1572872 | tf_op jit(solution)/shard_map/while/body/eval_jaxpr/ppermute | solution.py:19
  211.4 10.7 %collective-permute-start = (bf16[256,1024]{0,1:T(8,128)(2,1)}, bf16[256,1024]{0,1:T(8,128)(2,1)S(1)}, u32[]{:S(2)}, u32[]{:S(2)}) collective-permute-start(bf16[256,1024]{0,1:T(8,128)(2,1)} %get-tuple-element.507), channel_id=1, source_target_pairs={{0,4},{4,8},{8,12},{12,16},{16,20},{20,24},{24,28},{28,32},{32,36}... | collective-permute-start | bytes 1572872 | tf_op jit(solution)/shard_map/while/body/eval_jaxpr/ppermute | solution.py:19
  222.9 10.7 %collective-permute-start = (bf16[256,1024]{0,1:T(8,128)(2,1)}, bf16[256,1024]{0,1:T(8,128)(2,1)S(1)}, u32[]{:S(2)}, u32[]{:S(2)}) collective-permute-start(bf16[256,1024]{0,1:T(8,128)(2,1)} %get-tuple-element.507), channel_id=1, source_target_pairs={{0,4},{4,8},{8,12},{12,16},{16,20},{20,24},{24,28},{28,32},{32,36}... | collective-permute-start | bytes 1572872 | tf_op jit(solution)/shard_map/while/body/eval_jaxpr/ppermute | solution.py:19
  234.4 10.7 %collective-permute-start = (bf16[256,1024]{0,1:T(8,128)(2,1)}, bf16[256,1024]{0,1:T(8,128)(2,1)S(1)}, u32[]{:S(2)}, u32[]{:S(2)}) collective-permute-start(bf16[256,1024]{0,1:T(8,128)(2,1)} %get-tuple-element.507), channel_id=1, source_target_pairs={{0,4},{4,8},{8,12},{12,16},{16,20},{20,24},{24,28},{28,32},{32,36}... | collective-permute-start | bytes 1572872 | tf_op jit(solution)/shard_map/while/body/eval_jaxpr/ppermute | solution.py:19
  245.9 10.7 %collective-permute-start = (bf16[256,1024]{0,1:T(8,128)(2,1)}, bf16[256,1024]{0,1:T(8,128)(2,1)S(1)}, u32[]{:S(2)}, u32[]{:S(2)}) collective-permute-start(bf16[256,1024]{0,1:T(8,128)(2,1)} %get-tuple-element.507), channel_id=1, source_target_pairs={{0,4},{4,8},{8,12},{12,16},{16,20},{20,24},{24,28},{28,32},{32,36}... | collective-permute-start | bytes 1572872 | tf_op jit(solution)/shard_map/while/body/eval_jaxpr/ppermute | solution.py:19
  268.8 12.5 %collective-permute-start = (bf16[256,1024]{0,1:T(8,128)(2,1)}, bf16[256,1024]{0,1:T(8,128)(2,1)S(1)}, u32[]{:S(2)}, u32[]{:S(2)}) collective-permute-start(bf16[256,1024]{0,1:T(8,128)(2,1)} %get-tuple-element.507), channel_id=1, source_target_pairs={{0,4},{4,8},{8,12},{12,16},{16,20},{20,24},{24,28},{28,32},{32,36}... | collective-permute-start | bytes 1572872 | tf_op jit(solution)/shard_map/while/body/eval_jaxpr/ppermute | solution.py:19
  282.1 12.8 %collective-permute-start = (bf16[256,1024]{0,1:T(8,128)(2,1)}, bf16[256,1024]{0,1:T(8,128)(2,1)S(1)}, u32[]{:S(2)}, u32[]{:S(2)}) collective-permute-start(bf16[256,1024]{0,1:T(8,128)(2,1)} %get-tuple-element.507), channel_id=1, source_target_pairs={{0,4},{4,8},{8,12},{12,16},{16,20},{20,24},{24,28},{28,32},{32,36}... | collective-permute-start | bytes 1572872 | tf_op jit(solution)/shard_map/while/body/eval_jaxpr/ppermute | solution.py:19
  295.7 12.8 %collective-permute-start = (bf16[256,1024]{0,1:T(8,128)(2,1)}, bf16[256,1024]{0,1:T(8,128)(2,1)S(1)}, u32[]{:S(2)}, u32[]{:S(2)}) collective-permute-start(bf16[256,1024]{0,1:T(8,128)(2,1)} %get-tuple-element.507), channel_id=1, source_target_pairs={{0,4},{4,8},{8,12},{12,16},{16,20},{20,24},{24,28},{28,32},{32,36}... | collective-permute-start | bytes 1572872 | tf_op jit(solution)/shard_map/while/body/eval_jaxpr/ppermute | solution.py:19
  309.3 12.8 %collective-permute-start = (bf16[256,1024]{0,1:T(8,128)(2,1)}, bf16[256,1024]{0,1:T(8,128)(2,1)S(1)}, u32[]{:S(2)}, u32[]{:S(2)}) collective-permute-start(bf16[256,1024]{0,1:T(8,128)(2,1)} %get-tuple-element.507), channel_id=1, source_target_pairs={{0,4},{4,8},{8,12},{12,16},{16,20},{20,24},{24,28},{28,32},{32,36}... | collective-permute-start | bytes 1572872 | tf_op jit(solution)/shard_map/while/body/eval_jaxpr/ppermute | solution.py:19
  322.9 12.8 %collective-permute-start = (bf16[256,1024]{0,1:T(8,128)(2,1)}, bf16[256,1024]{0,1:T(8,128)(2,1)S(1)}, u32[]{:S(2)}, u32[]{:S(2)}) collective-permute-start(bf16[256,1024]{0,1:T(8,128)(2,1)} %get-tuple-element.507), channel_id=1, source_target_pairs={{0,4},{4,8},{8,12},{12,16},{16,20},{20,24},{24,28},{28,32},{32,36}... | collective-permute-start | bytes 1572872 | tf_op jit(solution)/shard_map/while/body/eval_jaxpr/ppermute | solution.py:19
  336.5 12.8 %collective-permute-start = (bf16[256,1024]{0,1:T(8,128)(2,1)}, bf16[256,1024]{0,1:T(8,128)(2,1)S(1)}, u32[]{:S(2)}, u32[]{:S(2)}) collective-permute-start(bf16[256,1024]{0,1:T(8,128)(2,1)} %get-tuple-element.507), channel_id=1, source_target_pairs={{0,4},{4,8},{8,12},{12,16},{16,20},{20,24},{24,28},{28,32},{32,36}... | collective-permute-start | bytes 1572872 | tf_op jit(solution)/shard_map/while/body/eval_jaxpr/ppermute | solution.py:19
  350.1 12.8 %collective-permute-start = (bf16[256,1024]{0,1:T(8,128)(2,1)}, bf16[256,1024]{0,1:T(8,128)(2,1)S(1)}, u32[]{:S(2)}, u32[]{:S(2)}) collective-permute-start(bf16[256,1024]{0,1:T(8,128)(2,1)} %get-tuple-element.507), channel_id=1, source_target_pairs={{0,4},{4,8},{8,12},{12,16},{16,20},{20,24},{24,28},{28,32},{32,36}... | collective-permute-start | bytes 1572872 | tf_op jit(solution)/shard_map/while/body/eval_jaxpr/ppermute | solution.py:19
  363.7 12.8 %collective-permute-start = (bf16[256,1024]{0,1:T(8,128)(2,1)}, bf16[256,1024]{0,1:T(8,128)(2,1)S(1)}, u32[]{:S(2)}, u32[]{:S(2)}) collective-permute-start(bf16[256,1024]{0,1:T(8,128)(2,1)} %get-tuple-element.507), channel_id=1, source_target_pairs={{0,4},{4,8},{8,12},{12,16},{16,20},{20,24},{24,28},{28,32},{32,36}... | collective-permute-start | bytes 1572872 | tf_op jit(solution)/shard_map/while/body/eval_jaxpr/ppermute | solution.py:19
  377.3 12.8 %collective-permute-start = (bf16[256,1024]{0,1:T(8,128)(2,1)}, bf16[256,1024]{0,1:T(8,128)(2,1)S(1)}, u32[]{:S(2)}, u32[]{:S(2)}) collective-permute-start(bf16[256,1024]{0,1:T(8,128)(2,1)} %get-tuple-element.507), channel_id=1, source_target_pairs={{0,4},{4,8},{8,12},{12,16},{16,20},{20,24},{24,28},{28,32},{32,36}... | collective-permute-start | bytes 1572872 | tf_op jit(solution)/shard_map/while/body/eval_jaxpr/ppermute | solution.py:19
  390.9 12.8 %collective-permute-start = (bf16[256,1024]{0,1:T(8,128)(2,1)}, bf16[256,1024]{0,1:T(8,128)(2,1)S(1)}, u32[]{:S(2)}, u32[]{:S(2)}) collective-permute-start(bf16[256,1024]{0,1:T(8,128)(2,1)} %get-tuple-element.507), channel_id=1, source_target_pairs={{0,4},{4,8},{8,12},{12,16},{16,20},{20,24},{24,28},{28,32},{32,36}... | collective-permute-start | bytes 1572872 | tf_op jit(solution)/shard_map/while/body/eval_jaxpr/ppermute | solution.py:19
  404.5 12.8 %collective-permute-start = (bf16[256,1024]{0,1:T(8,128)(2,1)}, bf16[256,1024]{0,1:T(8,128)(2,1)S(1)}, u32[]{:S(2)}, u32[]{:S(2)}) collective-permute-start(bf16[256,1024]{0,1:T(8,128)(2,1)} %get-tuple-element.507), channel_id=1, source_target_pairs={{0,4},{4,8},{8,12},{12,16},{16,20},{20,24},{24,28},{28,32},{32,36}... | collective-permute-start | bytes 1572872 | tf_op jit(solution)/shard_map/while/body/eval_jaxpr/ppermute | solution.py:19
  418.1 12.8 %collective-permute-start = (bf16[256,1024]{0,1:T(8,128)(2,1)}, bf16[256,1024]{0,1:T(8,128)(2,1)S(1)}, u32[]{:S(2)}, u32[]{:S(2)}) collective-permute-start(bf16[256,1024]{0,1:T(8,128)(2,1)} %get-tuple-element.507), channel_id=1, source_target_pairs={{0,4},{4,8},{8,12},{12,16},{16,20},{20,24},{24,28},{28,32},{32,36}... | collective-permute-start | bytes 1572872 | tf_op jit(solution)/shard_map/while/body/eval_jaxpr/ppermute | solution.py:19
  431.7 13.0 %collective-permute-start = (bf16[256,1024]{0,1:T(8,128)(2,1)}, bf16[256,1024]{0,1:T(8,128)(2,1)S(1)}, u32[]{:S(2)}, u32[]{:S(2)}) collective-permute-start(bf16[256,1024]{0,1:T(8,128)(2,1)} %get-tuple-element.507), channel_id=1, source_target_pairs={{0,4},{4,8},{8,12},{12,16},{16,20},{20,24},{24,28},{28,32},{32,36}... | collective-permute-start | bytes 1572872 | tf_op jit(solution)/shard_map/while/body/eval_jaxpr/ppermute | solution.py:19
  (15 other events, 705.4 us)
Sparse Core Ops, SparseCore 0:
  449.7 228.7 all-reduce.1
where the time goes:
time: 693 us; the launch traced here: 688 us
  waiting for transfers between devices  387 us (56%)
  starting transfers between devices  174 us (25%)
  other arithmetic  41.3 us (6%)
  local copies, waits for them, and re-layouts  36.8 us (5%)
  loops' own time  19.4 us (3%)
  between operations  15 us (2%)
  matrix products  14.6 us (2%)
    psum x1, waiting for transfers between devices, on_device(): lax.psum(jnp.dot(merged, w_out, preferred_element_type=jnp.float32).astyp...  229 us
    ppermute x32, starting transfers between devices, shifted(): lax.ppermute(value, axis, [(source, source + steps) for source in range(f...  174 us
    ppermute x32, waiting for transfers between devices, shifted(): lax.ppermute(value, axis, [(source, source + steps) for source in range(f...  158 us
    reduce_or x32, other arithmetic, absorb(): return lax.cond(jnp.any(allowed), compute, keep, state)  25.6 us
    while x32, local copies, waits for them, and re-layouts  25.2 us
    another operation x1, loops' own time, on_device(): state, unused = lax.fori_loop(0, reach, turn, (state, own))  19.3 us
  transfers between devices with their start and end apart: 33, of which 33 were waited for; matrix products, arithmetic and copies ran while one was open for 4% of the time, Pallas kernels for 0%

commit v1 on v0

--- a/solution.py
+++ b/solution.py
@@ -111,14 +111,16 @@
         jnp.zeros((2, heads, rows), jnp.float32),
         jnp.zeros((2, heads, rows, VD), jnp.float32),
     )
+    arriving = shifted(own, "req", 1)
     state = absorb(start, own, first)
 
     def turn(step, carry):
         current, moving = carry
-        moving = shifted(moving, "req", 1)
-        return (absorb(current, moving, first - (step + 1) * rows), moving)
+        following = shifted(moving, "req", 1)
+        return (absorb(current, moving, first - (step + 1) * rows), following)
 
-    state, unused = lax.fori_loop(0, reach, turn, (state, own))
+    state, moving = lax.fori_loop(0, reach - 1, turn, (state, arriving))
+    state = absorb(state, moving, first - reach * rows)
     top, mass, acc = state
     attended = acc / mass[..., None]
     diff = attended[0] - lam[:, None, None] * attended[1]

time: 693 us -> 615 us (0.89)
  waiting for transfers between devices: 387 us -> 283 us
  local copies, waits for them, and re-layouts: 36.8 us -> 71.1 us
  starting transfers between devices: 174 us -> 165 us
    psum x1, waiting for transfers between devices: 229 us -> 135 us  [on_device(): lax.psum(jnp.dot(merged, w_out, preferred_element_type=jnp.float32).astyp...]
    while x33 -> x31, local copies, waits for them, and re-layouts: 26.8 us -> 57.9 us
    ppermute x32, waiting for transfers between devices: 158 us -> 148 us  [shifted(): lax.ppermute(value, axis, [(source, source + steps) for source in range(f...]
    ppermute x32, starting transfers between devices: 174 us -> 165 us  [shifted(): lax.ppermute(value, axis, [(source, source + steps) for source in range(f...]
    reduce_or x32 -> x31, other arithmetic: 25.6 us -> 24.8 us  [absorb(): return lax.cond(jnp.any(allowed), compute, keep, state)]
  transfers between devices with their start and end apart: 33 -> 33, of which waited for: 33 -> 32; matrix products, arithmetic and copies ran while one was open for 4% -> 7% of each run, Pallas kernels for 0% -> 0%
where the time goes in v1:
time: 615 us; the launch traced here: 609 us
  waiting for transfers between devices  283 us (46%)
  starting transfers between devices  165 us (27%)
  local copies, waits for them, and re-layouts  71.1 us (12%)
  other arithmetic  43.3 us (7%)
  loops' own time  19.5 us (3%)
  between operations  15.7 us (3%)
  matrix products  12.3 us (2%)
    ppermute x32, starting transfers between devices, shifted(): lax.ppermute(value, axis, [(source, source + steps) for source in range(f...  165 us
    ppermute x32, waiting for transfers between devices, shifted(): lax.ppermute(value, axis, [(source, source + steps) for source in range(f...  148 us
    psum x1, waiting for transfers between devices, on_device(): lax.psum(jnp.dot(merged, w_out, preferred_element_type=jnp.float32).astyp...  135 us
    while x31, local copies, waits for them, and re-layouts  57.9 us
    reduce_or x31, other arithmetic, absorb(): return lax.cond(jnp.any(allowed), compute, keep, state)  24.8 us
    another operation x1, loops' own time, on_device(): state, moving = lax.fori_loop(0, reach - 1, turn, (state, arriving))  19 us
  transfers between devices with their start and end apart: 33, of which 32 were waited for; matrix products, arithmetic and copies ran while one was open for 7% of the time, Pallas kernels for 0%

profile of v1, /device:TPU:1, one launch (start us, length us, event | category | flops | bytes accessed | tf_op | source)
XLA Modules:
  0.0 609.4 jit_solution(146816331163059637)
XLA Ops:
  32.9 7.5 %conditional.3 = (f32[2,2,256]{2,1,0:T(2,128)}, f32[2,2,256]{2,1,0:T(2,128)S(1)}, f32[2,2,256,256]{3,2,0,1:T(8,128)S(1)}) conditional(s32[]{:T(128)} %convert_element_type.87, () %tuple.51, (pred[256,256]{0,1:T(8,128)(4,1)S(1)}, bf16[256,2,2,128]{3,0,1,2:T(8,128)(2,1)S(1)}, bf16[256,2,2,128]{3,0,1,2:T(8,128)(2,1)}, bf16[256,512]{1,0:T(8,128)(2,1)}) %tuple.125), branch_computations={%region_7.8_spmd, %region_8.11_spmd} | conditional | flops 203427840 | bytes 5685272 | solution.py:107
  42.7 417.4 %while.23 = (s32[]{:T(128)}, f32[2,2,256]{2,1,0:T(2,128)}, f32[2,2,256]{2,1,0:T(2,128)S(1)}, f32[2,2,256,256]{3,2,0,1:T(8,128)S(1)}, bf16[256,1024]{0,1:T(8,128)...) while((s32[]{:T(128)}, f32[2,2,256]{2,1,0:T(2,128)}, ...), condition=%wide.region_19.20_spmd.clone.clone, body=%wide.region_12.19_spmd.clone.clone.sunk | while | flops 204019456 | bytes 10498871 | solution.py:122
  60.7 4.9 collective-permute-done
  73.3 4.9 collective-permute-done
  86.0 4.9 collective-permute-done
  111.4 4.9 collective-permute-done
  136.7 4.9 collective-permute-done
  162.1 4.9 collective-permute-done
  187.4 4.9 collective-permute-done
  212.8 4.9 collective-permute-done
  238.1 4.9 collective-permute-done
  263.5 4.9 collective-permute-done
  270.2 6.0 collective-permute-start
  284.5 6.5 %collective-permute-start = (bf16[256,1024]{0,1:T(8,128)(2,1)}, bf16[256,1024]{0,1:T(8,128)(2,1)}, u32[]{:S(2)}, u32[]{:S(2)}) collective-permute-start(bf16[256,1024]{0,1:T(8,128)(2,1)} %copy.132), channel_id=1, source_target_pairs={{0,4},{4,8},{8,12},{12,16},{16,20},{20,24},{24,28},{28,32},{32,36}... | collective-permute-start | bytes 1572872 | tf_op jit(solution)/shard_map/while/body/eval_jaxpr/ppermute | solution.py:19
  292.5 4.9 collective-permute-done
  299.3 6.5 %collective-permute-start = (bf16[256,1024]{0,1:T(8,128)(2,1)}, bf16[256,1024]{0,1:T(8,128)(2,1)}, u32[]{:S(2)}, u32[]{:S(2)}) collective-permute-start(bf16[256,1024]{0,1:T(8,128)(2,1)} %copy.132), channel_id=1, source_target_pairs={{0,4},{4,8},{8,12},{12,16},{16,20},{20,24},{24,28},{28,32},{32,36}... | collective-permute-start | bytes 1572872 | tf_op jit(solution)/shard_map/while/body/eval_jaxpr/ppermute | solution.py:19
  307.3 4.9 collective-permute-done
  314.1 6.5 %collective-permute-start = (bf16[256,1024]{0,1:T(8,128)(2,1)}, bf16[256,1024]{0,1:T(8,128)(2,1)}, u32[]{:S(2)}, u32[]{:S(2)}) collective-permute-start(bf16[256,1024]{0,1:T(8,128)(2,1)} %copy.132), channel_id=1, source_target_pairs={{0,4},{4,8},{8,12},{12,16},{16,20},{20,24},{24,28},{28,32},{32,36}... | collective-permute-start | bytes 1572872 | tf_op jit(solution)/shard_map/while/body/eval_jaxpr/ppermute | solution.py:19
  322.1 4.9 collective-permute-done
  328.9 6.5 %collective-permute-start = (bf16[256,1024]{0,1:T(8,128)(2,1)}, bf16[256,1024]{0,1:T(8,128)(2,1)}, u32[]{:S(2)}, u32[]{:S(2)}) collective-permute-start(bf16[256,1024]{0,1:T(8,128)(2,1)} %copy.132), channel_id=1, source_target_pairs={{0,4},{4,8},{8,12},{12,16},{16,20},{20,24},{24,28},{28,32},{32,36}... | collective-permute-start | bytes 1572872 | tf_op jit(solution)/shard_map/while/body/eval_jaxpr/ppermute | solution.py:19
  343.7 6.5 %collective-permute-start = (bf16[256,1024]{0,1:T(8,128)(2,1)}, bf16[256,1024]{0,1:T(8,128)(2,1)}, u32[]{:S(2)}, u32[]{:S(2)}) collective-permute-start(bf16[256,1024]{0,1:T(8,128)(2,1)} %copy.132), channel_id=1, source_target_pairs={{0,4},{4,8},{8,12},{12,16},{16,20},{20,24},{24,28},{28,32},{32,36}... | collective-permute-start | bytes 1572872 | tf_op jit(solution)/shard_map/while/body/eval_jaxpr/ppermute | solution.py:19
  351.7 4.9 collective-permute-done
  358.4 6.5 %collective-permute-start = (bf16[256,1024]{0,1:T(8,128)(2,1)}, bf16[256,1024]{0,1:T(8,128)(2,1)}, u32[]{:S(2)}, u32[]{:S(2)}) collective-permute-start(bf16[256,1024]{0,1:T(8,128)(2,1)} %copy.132), channel_id=1, source_target_pairs={{0,4},{4,8},{8,12},{12,16},{16,20},{20,24},{24,28},{28,32},{32,36}... | collective-permute-start | bytes 1572872 | tf_op jit(solution)/shard_map/while/body/eval_jaxpr/ppermute | solution.py:19
  366.5 4.9 collective-permute-done
  373.2 6.5 %collective-permute-start = (bf16[256,1024]{0,1:T(8,128)(2,1)}, bf16[256,1024]{0,1:T(8,128)(2,1)}, u32[]{:S(2)}, u32[]{:S(2)}) collective-permute-start(bf16[256,1024]{0,1:T(8,128)(2,1)} %copy.132), channel_id=1, source_target_pairs={{0,4},{4,8},{8,12},{12,16},{16,20},{20,24},{24,28},{28,32},{32,36}... | collective-permute-start | bytes 1572872 | tf_op jit(solution)/shard_map/while/body/eval_jaxpr/ppermute | solution.py:19
  381.2 4.9 collective-permute-done
  388.0 6.5 %collective-permute-start = (bf16[256,1024]{0,1:T(8,128)(2,1)}, bf16[256,1024]{0,1:T(8,128)(2,1)}, u32[]{:S(2)}, u32[]{:S(2)}) collective-permute-start(bf16[256,1024]{0,1:T(8,128)(2,1)} %copy.132), channel_id=1, source_target_pairs={{0,4},{4,8},{8,12},{12,16},{16,20},{20,24},{24,28},{28,32},{32,36}... | collective-permute-start | bytes 1572872 | tf_op jit(solution)/shard_map/while/body/eval_jaxpr/ppermute | solution.py:19
  402.8 6.5 %collective-permute-start = (bf16[256,1024]{0,1:T(8,128)(2,1)}, bf16[256,1024]{0,1:T(8,128)(2,1)}, u32[]{:S(2)}, u32[]{:S(2)}) collective-permute-start(bf16[256,1024]{0,1:T(8,128)(2,1)} %copy.132), channel_id=1, source_target_pairs={{0,4},{4,8},{8,12},{12,16},{16,20},{20,24},{24,28},{28,32},{32,36}... | collective-permute-start | bytes 1572872 | tf_op jit(solution)/shard_map/while/body/eval_jaxpr/ppermute | solution.py:19
  417.6 6.5 %collective-permute-start = (bf16[256,1024]{0,1:T(8,128)(2,1)}, bf16[256,1024]{0,1:T(8,128)(2,1)}, u32[]{:S(2)}, u32[]{:S(2)}) collective-permute-start(bf16[256,1024]{0,1:T(8,128)(2,1)} %copy.132), channel_id=1, source_target_pairs={{0,4},{4,8},{8,12},{12,16},{16,20},{20,24},{24,28},{28,32},{32,36}... | collective-permute-start | bytes 1572872 | tf_op jit(solution)/shard_map/while/body/eval_jaxpr/ppermute | solution.py:19
  432.4 6.5 %collective-permute-start = (bf16[256,1024]{0,1:T(8,128)(2,1)}, bf16[256,1024]{0,1:T(8,128)(2,1)}, u32[]{:S(2)}, u32[]{:S(2)}) collective-permute-start(bf16[256,1024]{0,1:T(8,128)(2,1)} %copy.132), channel_id=1, source_target_pairs={{0,4},{4,8},{8,12},{12,16},{16,20},{20,24},{24,28},{28,32},{32,36}... | collective-permute-start | bytes 1572872 | tf_op jit(solution)/shard_map/while/body/eval_jaxpr/ppermute | solution.py:19
  447.1 6.5 %collective-permute-start = (bf16[256,1024]{0,1:T(8,128)(2,1)}, bf16[256,1024]{0,1:T(8,128)(2,1)}, u32[]{:S(2)}, u32[]{:S(2)}) collective-permute-start(bf16[256,1024]{0,1:T(8,128)(2,1)} %copy.132), channel_id=1, source_target_pairs={{0,4},{4,8},{8,12},{12,16},{16,20},{20,24},{24,28},{28,32},{32,36}... | collective-permute-start | bytes 1572872 | tf_op jit(solution)/shard_map/while/body/eval_jaxpr/ppermute | solution.py:19
  464.8 135.1 %all-reduce.2.cloned.1.call-done = bf16[256,2048]{1,0:T(8,128)(2,1)} async-done(((bf16[256,2048]{1,0:T(8,128)(2,1)}), bf16[256,2048]{1,0:T(8,128)(2,1)}) %all-reduce.2.cloned.1.call-update) | async-done | bytes 1048592 | tf_op jit(solution)/shard_map/psum | solution.py:134
  (337 shorter events, 282.9 us)
Async XLA Ops:
  7.2 592.7 %all-reduce.2.cloned.1.call-start = ((), (), s32[]{:S(2)}) async-start(), calls=%async_computation | async-start | bytes 2097152 | tf_op jit(solution)/shard_map/psum | solution.py:134
  21.9 18.7 %collective-permute-start.1 = (bf16[256,1024]{1,0:T(8,128)(2,1)}, bf16[256,1024]{1,0:T(8,128)(2,1)}, u32[]{:S(2)}, u32[]{:S(2)}) collective-permute-start(bf16[256,1024]{1,0:T(8,128)(2,1)} %pad_maximum_fusion), channel_id=1, source_target_pairs={{0,4},{4,8},{8,12},{12,16},{16,20},{20,24},{24,28},{28,32},{32,36}... | collective-permute-start | bytes 1572872 | tf_op jit(solution)/shard_map/ppermute | solution.py:19
  54.8 10.8 %collective-permute-start = (bf16[256,1024]{0,1:T(8,128)(2,1)}, bf16[256,1024]{0,1:T(8,128)(2,1)}, u32[]{:S(2)}, u32[]{:S(2)}) collective-permute-start(bf16[256,1024]{0,1:T(8,128)(2,1)} %copy.132), channel_id=1, source_target_pairs={{0,4},{4,8},{8,12},{12,16},{16,20},{20,24},{24,28},{28,32},{32,36}... | collective-permute-start | bytes 1572872 | tf_op jit(solution)/shard_map/while/body/eval_jaxpr/ppermute | solution.py:19
  67.4 10.8 %collective-permute-start = (bf16[256,1024]{0,1:T(8,128)(2,1)}, bf16[256,1024]{0,1:T(8,128)(2,1)}, u32[]{:S(2)}, u32[]{:S(2)}) collective-permute-start(bf16[256,1024]{0,1:T(8,128)(2,1)} %copy.132), channel_id=1, source_target_pairs={{0,4},{4,8},{8,12},{12,16},{16,20},{20,24},{24,28},{28,32},{32,36}... | collective-permute-start | bytes 1572872 | tf_op jit(solution)/shard_map/while/body/eval_jaxpr/ppermute | solution.py:19
  80.1 10.8 %collective-permute-start = (bf16[256,1024]{0,1:T(8,128)(2,1)}, bf16[256,1024]{0,1:T(8,128)(2,1)}, u32[]{:S(2)}, u32[]{:S(2)}) collective-permute-start(bf16[256,1024]{0,1:T(8,128)(2,1)} %copy.132), channel_id=1, source_target_pairs={{0,4},{4,8},{8,12},{12,16},{16,20},{20,24},{24,28},{28,32},{32,36}... | collective-permute-start | bytes 1572872 | tf_op jit(solution)/shard_map/while/body/eval_jaxpr/ppermute | solution.py:19
  92.8 10.8 %collective-permute-start = (bf16[256,1024]{0,1:T(8,128)(2,1)}, bf16[256,1024]{0,1:T(8,128)(2,1)}, u32[]{:S(2)}, u32[]{:S(2)}) collective-permute-start(bf16[256,1024]{0,1:T(8,128)(2,1)} %copy.132), channel_id=1, source_target_pairs={{0,4},{4,8},{8,12},{12,16},{16,20},{20,24},{24,28},{28,32},{32,36}... | collective-permute-start | bytes 1572872 | tf_op jit(solution)/shard_map/while/body/eval_jaxpr/ppermute | solution.py:19
  105.5 10.8 %collective-permute-start = (bf16[256,1024]{0,1:T(8,128)(2,1)}, bf16[256,1024]{0,1:T(8,128)(2,1)}, u32[]{:S(2)}, u32[]{:S(2)}) collective-permute-start(bf16[256,1024]{0,1:T(8,128)(2,1)} %copy.132), channel_id=1, source_target_pairs={{0,4},{4,8},{8,12},{12,16},{16,20},{20,24},{24,28},{28,32},{32,36}... | collective-permute-start | bytes 1572872 | tf_op jit(solution)/shard_map/while/body/eval_jaxpr/ppermute | solution.py:19
  118.1 10.8 %collective-permute-start = (bf16[256,1024]{0,1:T(8,128)(2,1)}, bf16[256,1024]{0,1:T(8,128)(2,1)}, u32[]{:S(2)}, u32[]{:S(2)}) collective-permute-start(bf16[256,1024]{0,1:T(8,128)(2,1)} %copy.132), channel_id=1, source_target_pairs={{0,4},{4,8},{8,12},{12,16},{16,20},{20,24},{24,28},{28,32},{32,36}... | collective-permute-start | bytes 1572872 | tf_op jit(solution)/shard_map/while/body/eval_jaxpr/ppermute | solution.py:19
  130.8 10.8 %collective-permute-start = (bf16[256,1024]{0,1:T(8,128)(2,1)}, bf16[256,1024]{0,1:T(8,128)(2,1)}, u32[]{:S(2)}, u32[]{:S(2)}) collective-permute-start(bf16[256,1024]{0,1:T(8,128)(2,1)} %copy.132), channel_id=1, source_target_pairs={{0,4},{4,8},{8,12},{12,16},{16,20},{20,24},{24,28},{28,32},{32,36}... | collective-permute-start | bytes 1572872 | tf_op jit(solution)/shard_map/while/body/eval_jaxpr/ppermute | solution.py:19
  143.5 10.8 %collective-permute-start = (bf16[256,1024]{0,1:T(8,128)(2,1)}, bf16[256,1024]{0,1:T(8,128)(2,1)}, u32[]{:S(2)}, u32[]{:S(2)}) collective-permute-start(bf16[256,1024]{0,1:T(8,128)(2,1)} %copy.132), channel_id=1, source_target_pairs={{0,4},{4,8},{8,12},{12,16},{16,20},{20,24},{24,28},{28,32},{32,36}... | collective-permute-start | bytes 1572872 | tf_op jit(solution)/shard_map/while/body/eval_jaxpr/ppermute | solution.py:19
  156.2 10.8 %collective-permute-start = (bf16[256,1024]{0,1:T(8,128)(2,1)}, bf16[256,1024]{0,1:T(8,128)(2,1)}, u32[]{:S(2)}, u32[]{:S(2)}) collective-permute-start(bf16[256,1024]{0,1:T(8,128)(2,1)} %copy.132), channel_id=1, source_target_pairs={{0,4},{4,8},{8,12},{12,16},{16,20},{20,24},{24,28},{28,32},{32,36}... | collective-permute-start | bytes 1572872 | tf_op jit(solution)/shard_map/while/body/eval_jaxpr/ppermute | solution.py:19
  168.8 10.8 %collective-permute-start = (bf16[256,1024]{0,1:T(8,128)(2,1)}, bf16[256,1024]{0,1:T(8,128)(2,1)}, u32[]{:S(2)}, u32[]{:S(2)}) collective-permute-start(bf16[256,1024]{0,1:T(8,128)(2,1)} %copy.132), channel_id=1, source_target_pairs={{0,4},{4,8},{8,12},{12,16},{16,20},{20,24},{24,28},{28,32},{32,36}... | collective-permute-start | bytes 1572872 | tf_op jit(solution)/shard_map/while/body/eval_jaxpr/ppermute | solution.py:19
  181.5 10.8 %collective-permute-start = (bf16[256,1024]{0,1:T(8,128)(2,1)}, bf16[256,1024]{0,1:T(8,128)(2,1)}, u32[]{:S(2)}, u32[]{:S(2)}) collective-permute-start(bf16[256,1024]{0,1:T(8,128)(2,1)} %copy.132), channel_id=1, source_target_pairs={{0,4},{4,8},{8,12},{12,16},{16,20},{20,24},{24,28},{28,32},{32,36}... | collective-permute-start | bytes 1572872 | tf_op jit(solution)/shard_map/while/body/eval_jaxpr/ppermute | solution.py:19
  194.2 10.8 %collective-permute-start = (bf16[256,1024]{0,1:T(8,128)(2,1)}, bf16[256,1024]{0,1:T(8,128)(2,1)}, u32[]{:S(2)}, u32[]{:S(2)}) collective-permute-start(bf16[256,1024]{0,1:T(8,128)(2,1)} %copy.132), channel_id=1, source_target_pairs={{0,4},{4,8},{8,12},{12,16},{16,20},{20,24},{24,28},{28,32},{32,36}... | collective-permute-start | bytes 1572872 | tf_op jit(solution)/shard_map/while/body/eval_jaxpr/ppermute | solution.py:19
  206.9 10.8 %collective-permute-start = (bf16[256,1024]{0,1:T(8,128)(2,1)}, bf16[256,1024]{0,1:T(8,128)(2,1)}, u32[]{:S(2)}, u32[]{:S(2)}) collective-permute-start(bf16[256,1024]{0,1:T(8,128)(2,1)} %copy.132), channel_id=1, source_target_pairs={{0,4},{4,8},{8,12},{12,16},{16,20},{20,24},{24,28},{28,32},{32,36}... | collective-permute-start | bytes 1572872 | tf_op jit(solution)/shard_map/while/body/eval_jaxpr/ppermute | solution.py:19
  219.5 10.8 %collective-permute-start = (bf16[256,1024]{0,1:T(8,128)(2,1)}, bf16[256,1024]{0,1:T(8,128)(2,1)}, u32[]{:S(2)}, u32[]{:S(2)}) collective-permute-start(bf16[256,1024]{0,1:T(8,128)(2,1)} %copy.132), channel_id=1, source_target_pairs={{0,4},{4,8},{8,12},{12,16},{16,20},{20,24},{24,28},{28,32},{32,36}... | collective-permute-start | bytes 1572872 | tf_op jit(solution)/shard_map/while/body/eval_jaxpr/ppermute | solution.py:19
  232.2 10.8 %collective-permute-start = (bf16[256,1024]{0,1:T(8,128)(2,1)}, bf16[256,1024]{0,1:T(8,128)(2,1)}, u32[]{:S(2)}, u32[]{:S(2)}) collective-permute-start(bf16[256,1024]{0,1:T(8,128)(2,1)} %copy.132), channel_id=1, source_target_pairs={{0,4},{4,8},{8,12},{12,16},{16,20},{20,24},{24,28},{28,32},{32,36}... | collective-permute-start | bytes 1572872 | tf_op jit(solution)/shard_map/while/body/eval_jaxpr/ppermute | solution.py:19
  244.9 10.8 %collective-permute-start = (bf16[256,1024]{0,1:T(8,128)(2,1)}, bf16[256,1024]{0,1:T(8,128)(2,1)}, u32[]{:S(2)}, u32[]{:S(2)}) collective-permute-start(bf16[256,1024]{0,1:T(8,128)(2,1)} %copy.132), channel_id=1, source_target_pairs={{0,4},{4,8},{8,12},{12,16},{16,20},{20,24},{24,28},{28,32},{32,36}... | collective-permute-start | bytes 1572872 | tf_op jit(solution)/shard_map/while/body/eval_jaxpr/ppermute | solution.py:19
  257.6 10.8 %collective-permute-start = (bf16[256,1024]{0,1:T(8,128)(2,1)}, bf16[256,1024]{0,1:T(8,128)(2,1)}, u32[]{:S(2)}, u32[]{:S(2)}) collective-permute-start(bf16[256,1024]{0,1:T(8,128)(2,1)} %copy.132), channel_id=1, source_target_pairs={{0,4},{4,8},{8,12},{12,16},{16,20},{20,24},{24,28},{28,32},{32,36}... | collective-permute-start | bytes 1572872 | tf_op jit(solution)/shard_map/while/body/eval_jaxpr/ppermute | solution.py:19
  270.2 12.4 %collective-permute-start = (bf16[256,1024]{0,1:T(8,128)(2,1)}, bf16[256,1024]{0,1:T(8,128)(2,1)}, u32[]{:S(2)}, u32[]{:S(2)}) collective-permute-start(bf16[256,1024]{0,1:T(8,128)(2,1)} %copy.132), channel_id=1, source_target_pairs={{0,4},{4,8},{8,12},{12,16},{16,20},{20,24},{24,28},{28,32},{32,36}... | collective-permute-start | bytes 1572872 | tf_op jit(solution)/shard_map/while/body/eval_jaxpr/ppermute | solution.py:19
  284.5 12.9 %collective-permute-start = (bf16[256,1024]{0,1:T(8,128)(2,1)}, bf16[256,1024]{0,1:T(8,128)(2,1)}, u32[]{:S(2)}, u32[]{:S(2)}) collective-permute-start(bf16[256,1024]{0,1:T(8,128)(2,1)} %copy.132), channel_id=1, source_target_pairs={{0,4},{4,8},{8,12},{12,16},{16,20},{20,24},{24,28},{28,32},{32,36}... | collective-permute-start | bytes 1572872 | tf_op jit(solution)/shard_map/while/body/eval_jaxpr/ppermute | solution.py:19
  299.3 12.9 %collective-permute-start = (bf16[256,1024]{0,1:T(8,128)(2,1)}, bf16[256,1024]{0,1:T(8,128)(2,1)}, u32[]{:S(2)}, u32[]{:S(2)}) collective-permute-start(bf16[256,1024]{0,1:T(8,128)(2,1)} %copy.132), channel_id=1, source_target_pairs={{0,4},{4,8},{8,12},{12,16},{16,20},{20,24},{24,28},{28,32},{32,36}... | collective-permute-start | bytes 1572872 | tf_op jit(solution)/shard_map/while/body/eval_jaxpr/ppermute | solution.py:19
  314.1 12.9 %collective-permute-start = (bf16[256,1024]{0,1:T(8,128)(2,1)}, bf16[256,1024]{0,1:T(8,128)(2,1)}, u32[]{:S(2)}, u32[]{:S(2)}) collective-permute-start(bf16[256,1024]{0,1:T(8,128)(2,1)} %copy.132), channel_id=1, source_target_pairs={{0,4},{4,8},{8,12},{12,16},{16,20},{20,24},{24,28},{28,32},{32,36}... | collective-permute-start | bytes 1572872 | tf_op jit(solution)/shard_map/while/body/eval_jaxpr/ppermute | solution.py:19
  328.9 12.9 %collective-permute-start = (bf16[256,1024]{0,1:T(8,128)(2,1)}, bf16[256,1024]{0,1:T(8,128)(2,1)}, u32[]{:S(2)}, u32[]{:S(2)}) collective-permute-start(bf16[256,1024]{0,1:T(8,128)(2,1)} %copy.132), channel_id=1, source_target_pairs={{0,4},{4,8},{8,12},{12,16},{16,20},{20,24},{24,28},{28,32},{32,36}... | collective-permute-start | bytes 1572872 | tf_op jit(solution)/shard_map/while/body/eval_jaxpr/ppermute | solution.py:19
  343.7 12.9 %collective-permute-start = (bf16[256,1024]{0,1:T(8,128)(2,1)}, bf16[256,1024]{0,1:T(8,128)(2,1)}, u32[]{:S(2)}, u32[]{:S(2)}) collective-permute-start(bf16[256,1024]{0,1:T(8,128)(2,1)} %copy.132), channel_id=1, source_target_pairs={{0,4},{4,8},{8,12},{12,16},{16,20},{20,24},{24,28},{28,32},{32,36}... | collective-permute-start | bytes 1572872 | tf_op jit(solution)/shard_map/while/body/eval_jaxpr/ppermute | solution.py:19
  358.4 12.9 %collective-permute-start = (bf16[256,1024]{0,1:T(8,128)(2,1)}, bf16[256,1024]{0,1:T(8,128)(2,1)}, u32[]{:S(2)}, u32[]{:S(2)}) collective-permute-start(bf16[256,1024]{0,1:T(8,128)(2,1)} %copy.132), channel_id=1, source_target_pairs={{0,4},{4,8},{8,12},{12,16},{16,20},{20,24},{24,28},{28,32},{32,36}... | collective-permute-start | bytes 1572872 | tf_op jit(solution)/shard_map/while/body/eval_jaxpr/ppermute | solution.py:19
  373.2 12.9 %collective-permute-start = (bf16[256,1024]{0,1:T(8,128)(2,1)}, bf16[256,1024]{0,1:T(8,128)(2,1)}, u32[]{:S(2)}, u32[]{:S(2)}) collective-permute-start(bf16[256,1024]{0,1:T(8,128)(2,1)} %copy.132), channel_id=1, source_target_pairs={{0,4},{4,8},{8,12},{12,16},{16,20},{20,24},{24,28},{28,32},{32,36}... | collective-permute-start | bytes 1572872 | tf_op jit(solution)/shard_map/while/body/eval_jaxpr/ppermute | solution.py:19
  388.0 12.9 %collective-permute-start = (bf16[256,1024]{0,1:T(8,128)(2,1)}, bf16[256,1024]{0,1:T(8,128)(2,1)}, u32[]{:S(2)}, u32[]{:S(2)}) collective-permute-start(bf16[256,1024]{0,1:T(8,128)(2,1)} %copy.132), channel_id=1, source_target_pairs={{0,4},{4,8},{8,12},{12,16},{16,20},{20,24},{24,28},{28,32},{32,36}... | collective-permute-start | bytes 1572872 | tf_op jit(solution)/shard_map/while/body/eval_jaxpr/ppermute | solution.py:19
  402.8 12.9 %collective-permute-start = (bf16[256,1024]{0,1:T(8,128)(2,1)}, bf16[256,1024]{0,1:T(8,128)(2,1)}, u32[]{:S(2)}, u32[]{:S(2)}) collective-permute-start(bf16[256,1024]{0,1:T(8,128)(2,1)} %copy.132), channel_id=1, source_target_pairs={{0,4},{4,8},{8,12},{12,16},{16,20},{20,24},{24,28},{28,32},{32,36}... | collective-permute-start | bytes 1572872 | tf_op jit(solution)/shard_map/while/body/eval_jaxpr/ppermute | solution.py:19
  417.6 12.9 %collective-permute-start = (bf16[256,1024]{0,1:T(8,128)(2,1)}, bf16[256,1024]{0,1:T(8,128)(2,1)}, u32[]{:S(2)}, u32[]{:S(2)}) collective-permute-start(bf16[256,1024]{0,1:T(8,128)(2,1)} %copy.132), channel_id=1, source_target_pairs={{0,4},{4,8},{8,12},{12,16},{16,20},{20,24},{24,28},{28,32},{32,36}... | collective-permute-start | bytes 1572872 | tf_op jit(solution)/shard_map/while/body/eval_jaxpr/ppermute | solution.py:19
  432.4 12.9 %collective-permute-start = (bf16[256,1024]{0,1:T(8,128)(2,1)}, bf16[256,1024]{0,1:T(8,128)(2,1)}, u32[]{:S(2)}, u32[]{:S(2)}) collective-permute-start(bf16[256,1024]{0,1:T(8,128)(2,1)} %copy.132), channel_id=1, source_target_pairs={{0,4},{4,8},{8,12},{12,16},{16,20},{20,24},{24,28},{28,32},{32,36}... | collective-permute-start | bytes 1572872 | tf_op jit(solution)/shard_map/while/body/eval_jaxpr/ppermute | solution.py:19
  447.1 12.9 %collective-permute-start = (bf16[256,1024]{0,1:T(8,128)(2,1)}, bf16[256,1024]{0,1:T(8,128)(2,1)}, u32[]{:S(2)}, u32[]{:S(2)}) collective-permute-start(bf16[256,1024]{0,1:T(8,128)(2,1)} %copy.132), channel_id=1, source_target_pairs={{0,4},{4,8},{8,12},{12,16},{16,20},{20,24},{24,28},{28,32},{32,36}... | collective-permute-start | bytes 1572872 | tf_op jit(solution)/shard_map/while/body/eval_jaxpr/ppermute | solution.py:19
  (16 other events, 659.5 us)
Sparse Core Ops, SparseCore 0:
  464.9 134.9 all-reduce.1

commit v2 on v0

v2 whole, which is shorter than its diff:
```python
import math

import jax
import jax.numpy as jnp
from jax import lax
from jax.sharding import Mesh
from jax.sharding import PartitionSpec as P

QK = 128
VD = 256
MAXLEN = 8192


lambda_start = 0.8 - 0.6 * math.exp(-3.3)
masked_score = -1e30


def locate(index, lengths):
    ends = jnp.cumsum(lengths)
    starts = ends - lengths
    segment = jnp.sum((ends[None, :] <= index[:, None]).astype(jnp.int32), axis=1)
    hit = jnp.arange(lengths.shape[0], dtype=jnp.int32)[None, :] == segment[:, None]
    begin = jnp.sum(jnp.where(hit, starts[None, :], 0), axis=1)
    return (segment, index - begin)


def rotate(proj, position):
    half = proj.shape[-1] // 2
    freq = 10000.0 ** (-jnp.arange(half, dtype=jnp.float32) / half)
    angle = position.astype(jnp.float32)[:, None] * freq[None, :]
    cosine = jnp.cos(angle)[:, None, None, :]
    sine = jnp.sin(angle)[:, None, None, :]
    front = proj[..., :half]
    back = proj[..., half:]
    return jnp.concatenate([front * cosine - back * sine, back * cosine + front * sine], axis=-1)


def swap_cores(value):
    return lax.ppermute(value, "core", [(0, 1), (1, 0)])


def on_device(tokens, norm_gain, w_query, w_key, w_value, w_out, lambdas, sub_gain, lengths):
    rows = tokens.shape[0]
    heads = w_query.shape[1] // (2 * QK)
    key_cols = heads * 2 * QK
    chips = lax.axis_size("chip")
    total = rows * 2 * chips
    core = lax.axis_index("core")
    chip = lax.axis_index("chip")
    first = (chip * 2 + core) * rows
    local_index = first + jnp.arange(rows, dtype=jnp.int32)
    unused, pos_own = locate(local_index, lengths)
    xf = tokens.astype(jnp.float32)
    normed = (xf * lax.rsqrt(jnp.mean(xf * xf, axis=-1, keepdims=True) + 1e-06) * norm_gain).astype(
        jnp.bfloat16
    )
    query = rotate(
        jnp.dot(normed, w_query, preferred_element_type=jnp.float32).reshape(rows, heads, 2, QK),
        pos_own,
    ).astype(jnp.bfloat16)
    keys = rotate(
        jnp.dot(normed, w_key, preferred_element_type=jnp.float32).reshape(rows, heads, 2, QK),
        pos_own,
    ).astype(jnp.bfloat16)
    values = jnp.dot(normed, w_value, preferred_element_type=jnp.float32).astype(jnp.bfloat16)
    key_flat = keys.reshape(rows, key_cols)
    lam = (
        jnp.exp(jnp.sum(lambdas[0] * lambdas[1], axis=-1))
        - jnp.exp(jnp.sum(lambdas[2] * lambdas[3], axis=-1))
        + lambda_start
    )
    scale = QK ** (-0.5)

    def head_part(h):
        q_h = lax.dynamic_index_in_dim(query, h, axis=1, keepdims=False).reshape(rows, 2 * QK)
        k_h = lax.dynamic_index_in_dim(keys, h, axis=1, keepdims=False).reshape(rows, 2 * QK)
        v_h = lax.dynamic_index_in_dim(values.reshape(rows, heads, VD), h, axis=1, keepdims=False)
        return jnp.concatenate([q_h, k_h, v_h], axis=1)

    mine = head_part(core)
    theirs = swap_cores(head_part(1 - core))
    pair = jnp.where(core == 0, jnp.concatenate([mine, theirs], axis=0), jnp.concatenate([theirs, mine], axis=0))
    span = 2 * rows
    q_pair = pair[:, : 2 * QK].reshape(span, 2, QK)
    kv_pair = pair[:, 2 * QK :]
    gathered = lax.all_gather(kv_pair, "chip", axis=0, tiled=True)

    window = min(MAXLEN + span, total)
    base = chip * span
    start = jnp.clip(base + span - window, 0, total - window)
    q_index = base + jnp.arange(span, dtype=jnp.int32)
    key_index = start + jnp.arange(window, dtype=jnp.int32)
    q_seg, unused = locate(q_index, lengths)
    k_seg, unused = locate(key_index, lengths)
    allowed = (key_index[None, :] <= q_index[:, None]) & (k_seg[None, :] == q_seg[:, None])
    kv_win = lax.dynamic_slice_in_dim(gathered, start, window, axis=0)
    v_win = kv_win[:, 2 * QK :]

    def attend(m):
        k_m = kv_win[:, m * QK : (m + 1) * QK]
        scores = jnp.einsum("qd,kd->qk", q_pair[:, m, :], k_m, preferred_element_type=jnp.float32) * scale
        scores = jnp.where(allowed, scores, masked_score)
        top = jnp.max(scores, axis=-1, keepdims=True)
        weights = jnp.where(allowed, jnp.exp(scores - top), 0.0)
        mass = jnp.sum(weights, axis=-1, keepdims=True)
        acc = jnp.dot(weights.astype(jnp.bfloat16), v_win, preferred_element_type=jnp.float32)
        return acc / mass

    lam_h = lax.dynamic_index_in_dim(lam, core, keepdims=False)
    gain_h = lax.dynamic_index_in_dim(sub_gain, core, axis=0, keepdims=False)
    diff = attend(0) - lam_h * attend(1)
    head_out = (
        diff * lax.rsqrt(jnp.mean(diff * diff, axis=-1, keepdims=True) + 1e-05) * gain_h * (1.0 - lambda_start)
    ).astype(jnp.bfloat16)
    own_rows = lax.dynamic_slice_in_dim(head_out, core * rows, rows, axis=0)
    other_rows = swap_cores(lax.dynamic_slice_in_dim(head_out, (1 - core) * rows, rows, axis=0))
    merged = jnp.where(
        core == 0,
        jnp.concatenate([own_rows, other_rows], axis=1),
        jnp.concatenate([other_rows, own_rows], axis=1),
    )
    summed = lax.psum(
        jnp.dot(merged, w_out, preferred_element_type=jnp.float32).astype(jnp.bfloat16), "tp"
    ).astype(jnp.float32)
    hidden = (xf + summed).astype(jnp.bfloat16)
    return (hidden, key_flat, values)


def solution(mesh):
    req, tp = mesh.shape["req"], mesh.shape["tp"]
    paired = Mesh(mesh.devices.reshape(req // 2, 2, tp), ("chip", "core", "tp"))
    rows = ("chip", "core")
    in_specs = (
        P(rows, None),
        P(),
        P(None, "tp"),
        P(None, "tp"),
        P(None, "tp"),
        P("tp", None),
        P(None, "tp", None),
        P("tp", None),
        P(),
    )
    out_specs = (P(rows, None), P(rows, "tp"), P(rows, "tp"))
    return jax.shard_map(
        on_device, mesh=paired, in_specs=in_specs, out_specs=out_specs, check_vma=False
    )
```

time: 693 us -> 393 us (0.57)
  starting transfers between devices: 174 us -> 9.75 us
  waiting for transfers between devices: 387 us -> 256 us
  matrix products: 14.6 us -> 83.7 us
  local copies, waits for them, and re-layouts: 36.8 us -> 5.88 us
  loops' own time: 19.4 us -> 0 us
  other arithmetic: 41.3 us -> 22.3 us
    all_gather x0 -> x1, waiting for transfers between devices: none -> 190 us  [on_device(): gathered = lax.all_gather(kv_pair, 'chip', axis=0, tiled=True)]
    psum x1, waiting for transfers between devices: 229 us -> 64 us  [on_device(): lax.psum(jnp.dot(merged, w_out, preferred_element_type=jnp.float32).astyp...]
    ppermute x32 -> x2, starting transfers between devices: 174 us -> 9.67 us  [swap_cores(): return lax.ppermute(value, 'core', [(0, 1), (1, 0)])]
    ppermute x32 -> x2, waiting for transfers between devices: 158 us -> 2.47 us  [swap_cores(): return lax.ppermute(value, 'core', [(0, 1), (1, 0)])]
    dot_general x4, matrix products: 4.67 us -> 73.1 us  [the longest x2 42.8 us: attend(): jnp.dot(weights.astype(jnp.bfloat16), v_win, preferred_element_type=jnp.f...]
    while x33 -> x0, local copies, waits for them, and re-layouts: 26.8 us -> none
    reduce_or x32 -> x0, other arithmetic: 25.6 us -> none  [absorb(): return lax.cond(jnp.any(allowed), compute, keep, state)]
    another operation x34 -> x0, loops' own time: 19.4 us -> none  [the longest x1 19.3 us: on_device(): state, unused = lax.fori_loop(0, reach, turn, (state, own))]
  transfers between devices with their start and end apart: 33 -> 4, of which waited for: 33 -> 4; matrix products, arithmetic and copies ran while one was open for 4% -> 1% of each run, Pallas kernels for 0% -> 0%
where the time goes in v2:
time: 393 us; the launch traced here: 392 us
  waiting for transfers between devices  256 us (65%)
  matrix products  83.7 us (21%)
  other arithmetic  22.3 us (6%)
  between operations  14.3 us (4%)
  starting transfers between devices  9.75 us (2%)
  local copies, waits for them, and re-layouts  5.88 us (1%)
    all_gather x1, waiting for transfers between devices, on_device(): gathered = lax.all_gather(kv_pair, 'chip', axis=0, tiled=True)  190 us
    psum x1, waiting for transfers between devices, on_device(): lax.psum(jnp.dot(merged, w_out, preferred_element_type=jnp.float32).astyp...  64 us
    dot_general x2, matrix products, attend(): jnp.dot(weights.astype(jnp.bfloat16), v_win, preferred_element_type=jnp.f...  42.8 us
    dot_general x2, matrix products, attend(): jnp.einsum('qd,kd->qk', q_pair[:, m, :], k_m, preferred_element_type=jnp....  30.4 us
    ppermute x2, starting transfers between devices, swap_cores(): return lax.ppermute(value, 'core', [(0, 1), (1, 0)])  9.67 us
    reduce_sum x1, other arithmetic, attend(): mass = jnp.sum(weights, axis=-1, keepdims=True)  9.22 us
  transfers between devices with their start and end apart: 4, of which 4 were waited for; matrix products, arithmetic and copies ran while one was open for 1% of the time, Pallas kernels for 0%

profile of v2, /device:TPU:1, one launch (start us, length us, event | category | flops | bytes accessed | tf_op | source)
XLA Modules:
  0.0 392.0 jit_solution(11088976838659435869)
XLA Ops:
  7.3 1.0 reduce-window.8
  8.3 0.7 bitcast_subtract_fusion
  9.1 1.5 fusion.16
  10.6 2.7 fusion.57
  13.7 3.5 fusion.59
  17.1 1.4 reshape.165
  18.5 0.5 multiply_cosine_fusion
  19.0 1.6 multiply_subtract_fusion
  20.6 0.8 add_convert_fusion
  21.4 1.7 maximum_convert_fusion
  23.2 0.9 fusion.47
  24.1 2.7 convolution_convert_fusion.1
  26.8 0.7 copy-done.2
  27.6 0.5 constant_dynamic-slice_fusion.5
  28.2 0.8 pad_maximum_fusion
  28.9 3.3 collective-permute-start
  32.3 1.5 collective-permute-done
  34.1 0.8 slice.66
  35.2 0.6 dynamic_slice.44
  36.1 0.4 fusion.61
  36.5 189.6 %all-gather.2.cloned.1.call-done = bf16[16384,512]{1,0:T(8,128)(2,1)} async-done(((bf16[512,512]{1,0:T(8,128)(2,1)}), bf16[16384,512]{1,0:T(8,128)(2,1)}) %all-gather.2.cloned.1.call-update) | async-done | bytes 16777232 | tf_op jit(solution)/shard_map/all_gather | solution.py:86
  226.1 11.1 %fusion = (f32[512]{0:T(512)S(1)}, f32[512,8704]{1,0:T(8,128)}) fusion(s32[512]{0:T(512)S(1)} %convert_reduce_fusion.1, s32[8704]{0:T(1024)S(1)} %convert_reduce_fusion, s32[512]{0:T(512)S(1)} %iota_add_fusion.1, s32[8704]{0:T(1024)S(1)} %iota_add_fusion, bf16[16384,512]{1,0:T(8,128)(2,1)} %all-gather.2.cloned.1.call-done, s32[]{:T(128)S(6)} %min.4, ...), kind=kOutput, calls=%fused_computation.5 | convolution fusion | flops 1167588864 | bytes 20260868 | tf_op jit(solution)/shard_map/qd,kd->qk/dot_general | solution.py:101
  237.1 19.3 %fusion.2 = (f32[512]{0:T(512)S(1)}, f32[512]{0:T(512)S(1)}, f32[512,8704]{1,0:T(8,128)}) fusion(f32[512,8704]{1,0:T(8,128)} %get-tuple-element.24, f32[512]{0:T(512)S(1)} %get-tuple-element.23, s32[512]{0:T(512)S(1)} %convert_reduce_fusion.1, s32[8704]{0:T(1024)S(1)} %convert_reduce_fusion, s32[512]{0:T(512)S(1)} %iota_add_fusion.1, ...), kind=kOutput, calls=%fused_computation.7 | convolution fusion | flops 1189870592 | bytes 38090760 | tf_op jit(solution)/shard_map/qd,kd->qk/dot_general | solution.py:101
  256.5 9.2 %fusion.4 = f32[512]{0:T(512)S(1)} fusion(f32[512,8704]{1,0:T(8,128)} %get-tuple-element.25, f32[512]{0:T(512)S(1)} %get-tuple-element.4, s32[512]{0:T(512)S(1)} %convert_reduce_fusion.1, s32[8704]{0:T(1024)S(1)} %convert_reduce_fusion, s32[512]{0:T(512)S(1)} %iota_add_fusion.1, s32[8704]{0:T(1024)S(1)} %iota_add_fusion), kind=kLoop, calls=%fused_computation.9 | loop fusion | flops 35651072 | bytes 17903616 | tf_op jit(solution)/shard_map/reduce_sum | solution.py:105
  265.7 21.6 %fusion.35 = f32[512,256]{0,1:T(8,128)S(1)} fusion(bf16[16384,512]{1,0:T(8,128)(2,1)} %all-gather.2.cloned.1.call-done, s32[]{:T(128)S(6)} %min.4, s32[]{:T(128)S(6)} %add.123, f32[512,8704]{1,0:T(8,128)} %get-tuple-element.25, f32[512]{0:T(512)S(1)} %get-tuple-element.4, f32[512]{0:T(512)S(1)} %fusion.4, f32[]{:T(128)} %bitcast.5, ...), kind=kOutput, calls=%fused_computation.31 | convolution fusion | flops 2317615104 | bytes 22884872 | tf_op jit(solution)/shard_map/dot_general | solution.py:106
  287.3 21.2 %multiply_reduce_fusion = (f32[512]{0:T(512)S(1)}, f32[512,256]{0,1:T(8,128)S(1)}) fusion(f32[512,256]{0,1:T(8,128)S(1)} %fusion.35, f32[512]{0:T(512)S(1)} %get-tuple-element.3, bf16[16384,512]{1,0:T(8,128)(2,1)} %all-gather.2.cloned.1.call-done, s32[]{:T(128)S(6)} %min.4, s32[]{:T(128)S(6)} %add.123, f32[512,8704]{1,0:T(8,128)} %get-tuple-element.24, ...), kind=kOutput, calls=%fused_computation.35 | convolution fusion | flops 2317876736 | bytes 23410696 | tf_op jit(solution)/shard_map/dot_general | solution.py:106
  308.6 6.4 %collective-permute-start.1 = (bf16[256,256]{0,1:T(8,128)(2,1)S(1)}, bf16[256,256]{0,1:T(8,128)(2,1)S(1)}, u32[]{:S(2)}, u32[]{:S(2)}) collective-permute-start(bf16[256,256]{0,1:T(8,128)(2,1)S(1)} %get-tuple-element.14), channel_id=1, source_target_pairs={{0,4},{4,0},{1,5},{5,1},{2,6},{6,2},{3,7},{7,3},{8,12},{12,8},{9,1... | collective-permute-start | bytes 393224 | tf_op jit(solution)/shard_map/ppermute | solution.py:39
  315.0 1.0 collective-permute-done.1
  316.0 1.7 convolution_convert_fusion
  317.8 0.8 convert_element_type.66
  318.6 64.0 %all-reduce.2.cloned.1.call-done = bf16[256,2048]{1,0:T(8,128)(2,1)} async-done(((bf16[256,2048]{1,0:T(8,128)(2,1)}), bf16[256,2048]{1,0:T(8,128)(2,1)}) %all-reduce.2.cloned.1.call-update) | async-done | bytes 1048592 | tf_op jit(solution)/shard_map/psum | solution.py:122
  382.6 2.6 fusion.19
  (42 shorter events, 1.8 us)
Async XLA Ops:
  7.2 308.9 %copy-start = (bf16[512,2048]{1,0:T(8,128)(2,1)S(1)}, bf16[512,2048]{1,0:T(8,128)(2,1)}, u32[]{:S(2)}) copy-start(bf16[512,2048]{1,0:T(8,128)(2,1)} %param.14) | copy-start | bytes 6291460
  7.2 16.9 %copy-start.5 = (f32[2048]{0:T(1024)S(1)}, f32[2048]{0:T(1024)}, u32[]{:S(2)}) copy-start(f32[2048]{0:T(1024)} %param.10) | copy-start | bytes 24580
  7.2 27.8 %copy-start.3 = (f32[4,2,128]{2,1,0:T(2,128)S(1)}, f32[4,2,128]{2,1,0:T(2,128)}, u32[]{:S(2)}) copy-start(f32[4,2,128]{2,1,0:T(2,128)} %param.15) | copy-start | bytes 12292
  7.2 28.6 %copy-start.4 = (f32[2,256]{1,0:T(2,128)S(1)}, f32[2,256]{1,0:T(2,128)}, u32[]{:S(2)}) copy-start(f32[2,256]{1,0:T(2,128)} %param.16) | copy-start | bytes 6148
  7.2 218.9 %all-gather.2.cloned.1.call-start = ((), (), s32[]{:S(2)}) async-start(), calls=%async_computation | async-start | bytes 17301504 | tf_op jit(solution)/shard_map/all_gather | solution.py:86
  26.8 0.7 copy-start.2
  28.9 4.8 %collective-permute-start = (bf16[256,768]{1,0:T(8,128)(2,1)}, bf16[256,768]{1,0:T(8,128)(2,1)S(1)}, u32[]{:S(2)}, u32[]{:S(2)}) collective-permute-start(bf16[256,768]{1,0:T(8,128)(2,1)} %pad_maximum_fusion), channel_id=1, source_target_pairs={{0,4},{4,0},{1,5},{5,1},{2,6},{6,2},{3,7},{7,3},{8,12},{12,8},{9,1... | collective-permute-start | bytes 1179656 | tf_op jit(solution)/shard_map/ppermute | solution.py:39
  34.9 347.7 %all-reduce.2.cloned.1.call-start = ((), (), s32[]{:S(2)}) async-start(), calls=%async_computation.1 | async-start | bytes 2097152 | tf_op jit(solution)/shard_map/psum | solution.py:122
  287.2 95.4 %copy-start.1 = (bf16[256,2048]{1,0:T(8,128)(2,1)S(1)}, bf16[256,2048]{1,0:T(8,128)(2,1)}, u32[]{:S(2)}) copy-start(bf16[256,2048]{1,0:T(8,128)(2,1)} %param.9) | copy-start | bytes 3145732
  308.6 7.4 %collective-permute-start.1 = (bf16[256,256]{0,1:T(8,128)(2,1)S(1)}, bf16[256,256]{0,1:T(8,128)(2,1)S(1)}, u32[]{:S(2)}, u32[]{:S(2)}) collective-permute-start(bf16[256,256]{0,1:T(8,128)(2,1)S(1)} %get-tuple-element.14), channel_id=1, source_target_pairs={{0,4},{4,0},{1,5},{5,1},{2,6},{6,2},{3,7},{7,3},{8,12},{12,8},{9,1... | collective-permute-start | bytes 393224 | tf_op jit(solution)/shard_map/ppermute | solution.py:39
Sparse Core Ops, SparseCore 0:
  35.1 190.9 all-gather.1
  317.9 64.6 all-reduce.1

commit v3 on v2

--- a/solution.py
+++ b/solution.py
@@ -82,29 +82,45 @@
     pair = jnp.where(core == 0, jnp.concatenate([mine, theirs], axis=0), jnp.concatenate([theirs, mine], axis=0))
     span = 2 * rows
     q_pair = pair[:, : 2 * QK].reshape(span, 2, QK)
-    kv_pair = pair[:, 2 * QK :]
-    gathered = lax.all_gather(kv_pair, "chip", axis=0, tiled=True)
+    own_gathered = lax.all_gather(mine[:, 2 * QK :], "chip", axis=0, tiled=True)
+    other_gathered = lax.all_gather(theirs[:, 2 * QK :], "chip", axis=0, tiled=True)
 
-    window = min(MAXLEN + span, total)
+    reach = min(MAXLEN // span + 1, chips)
+    first_chip = jnp.clip(chip + 1 - reach, 0, chips - reach)
     base = chip * span
-    start = jnp.clip(base + span - window, 0, total - window)
     q_index = base + jnp.arange(span, dtype=jnp.int32)
-    key_index = start + jnp.arange(window, dtype=jnp.int32)
     q_seg, unused = locate(q_index, lengths)
-    k_seg, unused = locate(key_index, lengths)
-    allowed = (key_index[None, :] <= q_index[:, None]) & (k_seg[None, :] == q_seg[:, None])
-    kv_win = lax.dynamic_slice_in_dim(gathered, start, window, axis=0)
-    v_win = kv_win[:, 2 * QK :]
+    slot = jnp.arange(reach * rows, dtype=jnp.int32)
+
+    def part(gathered, half):
+        key_index = (first_chip + slot // rows) * span + half * rows + slot % rows
+        k_seg, unused = locate(key_index, lengths)
+        allowed = (key_index[None, :] <= q_index[:, None]) & (k_seg[None, :] == q_seg[:, None])
+        kv_win = lax.dynamic_slice_in_dim(gathered, first_chip * rows, reach * rows, axis=0)
+        v_win = kv_win[:, 2 * QK :]
+        stats = []
+        for m in range(2):
+            k_m = kv_win[:, m * QK : (m + 1) * QK]
+            scores = jnp.einsum("qd,kd->qk", q_pair[:, m, :], k_m, preferred_element_type=jnp.float32) * scale
+            scores = jnp.where(allowed, scores, masked_score)
+            top = jnp.max(scores, axis=-1, keepdims=True)
+            weights = jnp.where(allowed, jnp.exp(scores - top), 0.0)
+            mass = jnp.sum(weights, axis=-1, keepdims=True)
+            acc = jnp.dot(weights.astype(jnp.bfloat16), v_win, preferred_element_type=jnp.float32)
+            stats.append((top, mass, acc))
+        return stats
+
+    own_stats = part(own_gathered, core)
+    own_stats, other_gathered = lax.optimization_barrier((own_stats, other_gathered))
+    other_stats = part(other_gathered, 1 - core)
 
     def attend(m):
-        k_m = kv_win[:, m * QK : (m + 1) * QK]
-        scores = jnp.einsum("qd,kd->qk", q_pair[:, m, :], k_m, preferred_element_type=jnp.float32) * scale
-        scores = jnp.where(allowed, scores, masked_score)
-        top = jnp.max(scores, axis=-1, keepdims=True)
-        weights = jnp.where(allowed, jnp.exp(scores - top), 0.0)
-        mass = jnp.sum(weights, axis=-1, keepdims=True)
-        acc = jnp.dot(weights.astype(jnp.bfloat16), v_win, preferred_element_type=jnp.float32)
-        return acc / mass
+        top_a, mass_a, acc_a = own_stats[m]
+        top_b, mass_b, acc_b = other_stats[m]
+        top = jnp.maximum(top_a, top_b)
+        fade_a = jnp.exp(top_a - top)
+        fade_b = jnp.exp(top_b - top)
+        return (acc_a * fade_a + acc_b * fade_b) / (mass_a * fade_a + mass_b * fade_b)
 
     lam_h = lax.dynamic_index_in_dim(lam, core, keepdims=False)
     gain_h = lax.dynamic_index_in_dim(sub_gain, core, axis=0, keepdims=False)

time: 393 us -> 472 us (1.20)
  waiting for transfers between devices: 256 us -> 369 us
  matrix products: 83.7 us -> 35.8 us
  starting transfers between devices: 9.75 us -> 23.1 us
    all_gather x1 -> x2, waiting for transfers between devices: 190 us -> 300 us  [the longest x1 155 us: on_device(): lax.all_gather(theirs[:, 2 * QK:], 'chip', axis=0, tiled=True)]
    dot_general x4 -> x8, matrix products: 73.1 us -> 25.2 us  [the longest x4 13 us: part(): jnp.einsum('qd,kd->qk', q_pair[:, m, :], k_m, preferred_element_type=jnp....]
    ppermute x2, starting transfers between devices: 9.67 us -> 22.8 us  [swap_cores(): return lax.ppermute(value, 'core', [(0, 1), (1, 0)])]
    reduce_sum x1 -> x2, other arithmetic: 9.22 us -> 10.4 us  [part(): mass = jnp.sum(weights, axis=-1, keepdims=True)]
  transfers between devices with their start and end apart: 4 -> 5, of which waited for: 4 -> 5; matrix products, arithmetic and copies ran while one was open for 1% -> 5% of each run, Pallas kernels for 0% -> 0%
where the time goes in v3:
time: 472 us
  waiting for transfers between devices  369 us (78%)
  matrix products  35.8 us (8%)
  starting transfers between devices  23.1 us (5%)
  other arithmetic  22 us (5%)
  between operations  14.2 us (3%)
  local copies, waits for them, and re-layouts  7.51 us (2%)
    all_gather x1, waiting for transfers between devices, on_device(): lax.all_gather(theirs[:, 2 * QK:], 'chip', axis=0, tiled=True)  155 us
    all_gather x1, waiting for transfers between devices, on_device(): own_gathered = lax.all_gather(mine[:, 2 * QK:], 'chip', axis=0, tiled=True)  145 us
    psum x1, waiting for transfers between devices, on_device(): lax.psum(jnp.dot(merged, w_out, preferred_element_type=jnp.float32).astyp...  67 us
    ppermute x2, starting transfers between devices, swap_cores(): return lax.ppermute(value, 'core', [(0, 1), (1, 0)])  22.8 us
    dot_general x4, matrix products, part(): jnp.einsum('qd,kd->qk', q_pair[:, m, :], k_m, preferred_element_type=jnp....  13 us
    dot_general x4, matrix products, part(): jnp.dot(weights.astype(jnp.bfloat16), v_win, preferred_element_type=jnp.f...  12.2 us
    reduce_sum x2, other arithmetic, part(): mass = jnp.sum(weights, axis=-1, keepdims=True)  10.4 us
  transfers between devices with their start and end apart: 5, of which 5 were waited for; matrix products, arithmetic and copies ran while one was open for 5% of the time, Pallas kernels for 0%

profile of v3, /device:TPU:1, one launch (start us, length us, event | category | flops | bytes accessed | tf_op | source)
XLA Modules:
  0.0 471.6 jit_solution(14739284118266827972)
XLA Ops:
  7.8 1.5 fusion.24
  9.4 2.7 convolution_convert_fusion.1
  12.2 1.2 constant_dynamic-slice_fusion.3
  13.4 2.7 fusion.112
  16.9 3.5 fusion.110
  20.3 1.4 reshape.216
  21.7 1.2 multiply_cosine_fusion
  22.9 0.8 add_convert_fusion
  23.7 0.8 multiply_subtract_fusion
  25.2 0.9 fusion.84
  27.0 1.0 copy.60
  28.0 3.3 collective-permute-start
  31.4 1.3 collective-permute-done
  35.4 0.8 convert_reduce_fusion
  36.8 144.8 %all-gather.3.cloned.1.call-done = bf16[8192,512]{1,0:T(8,128)(2,1)} async-done(((bf16[256,512]{1,0:T(8,128)(2,1)}), bf16[8192,512]{1,0:T(8,128)(2,1)}) %all-gather.3.cloned.1.call-update) | async-done | bytes 8388624 | tf_op jit(solution)/shard_map/all_gather | solution.py:85
  181.5 3.9 fusion.119
  185.5 2.6 fusion.120
  188.1 3.2 fusion.14
  191.4 3.2 fusion.12
  194.6 5.1 %fusion.3 = (f32[512]{0:T(512)S(1)}, f32[512]{0:T(512)S(1)}) fusion(f32[512,4352]{1,0:T(8,128)S(1)} %get-tuple-element.50, f32[512]{0:T(512)S(1)} %get-tuple-element.49, s32[512]{0:T(512)S(1)} %convert_reduce_fusion.2, s32[4352]{0:T(1024)S(1)} %copy-done.8, s32[512]{0:T(512)S(1)} %iota_add_fusion, s32[4352]{0:T(1024)S(1)} %copy-done.6, ...), kind=kLoop, calls=%fused_computation.13 | loop fusion | flops 20052992 | bytes 17872896 | tf_op jit(solution)/shard_map/reduce_sum | solution.py:108
  199.6 154.8 %all-gather.5.cloned.1.call-done = bf16[8192,512]{1,0:T(8,128)(2,1)} async-done(((bf16[256,512]{1,0:T(8,128)(2,1)}), bf16[8192,512]{1,0:T(8,128)(2,1)}) %all-gather.5.cloned.1.call-update) | async-done | bytes 8388624 | tf_op jit(solution)/shard_map/all_gather | solution.py:86
  354.4 3.9 fusion.121
  358.4 2.6 fusion.122
  361.0 5.4 %fusion.4 = (f32[512]{0:T(512)S(1)}, f32[512]{0:T(512)S(1)}) fusion(f32[512,4352]{1,0:T(8,128)S(1)} %get-tuple-element.54, f32[512]{0:T(512)S(1)} %get-tuple-element.53, s32[512]{0:T(512)S(1)} %convert_reduce_fusion.2, s32[4352]{0:T(1024)S(1)} %copy-done.7, s32[512]{0:T(512)S(1)} %iota_add_fusion, s32[4352]{0:T(1024)S(1)} %copy-done.4, ...), kind=kLoop, calls=%fused_computation.14 | loop fusion | flops 20052992 | bytes 17872896 | tf_op jit(solution)/shard_map/reduce_sum | solution.py:108
  366.4 3.2 fusion.71
  369.7 2.5 multiply_reduce_fusion
  372.4 19.5 %collective-permute-start.1 = (bf16[256,256]{1,0:T(8,128)(2,1)S(1)}, bf16[256,256]{1,0:T(8,128)(2,1)S(1)}, u32[]{:S(2)}, u32[]{:S(2)}) collective-permute-start(bf16[256,256]{1,0:T(8,128)(2,1)S(1)} %get-tuple-element.38), channel_id=1, source_target_pairs={{0,4},{4,0},{1,5},{5,1},{2,6},{6,2},{3,7},{7,3},{8,12},{12,8},{9,1... | collective-permute-start | bytes 393224 | tf_op jit(solution)/shard_map/ppermute | solution.py:39
  391.9 1.0 collective-permute-done.1
  392.9 1.7 convolution_convert_fusion
  394.6 0.8 convert_element_type.78
  395.4 67.0 %all-reduce.2.cloned.1.call-done = bf16[256,2048]{1,0:T(8,128)(2,1)} async-done(((bf16[256,2048]{1,0:T(8,128)(2,1)}), bf16[256,2048]{1,0:T(8,128)(2,1)}) %all-reduce.2.cloned.1.call-update) | async-done | bytes 1048592 | tf_op jit(solution)/shard_map/psum | solution.py:138
  462.4 2.6 fusion.27
  (77 shorter events, 6.5 us)
Async XLA Ops:
  7.2 385.7 %copy-start = (bf16[512,2048]{1,0:T(8,128)(2,1)S(1)}, bf16[512,2048]{1,0:T(8,128)(2,1)}, u32[]{:S(2)}) copy-start(bf16[512,2048]{1,0:T(8,128)(2,1)} %param.14) | copy-start | bytes 6291460
  7.2 9.3 %copy-start.10 = (s32[4]{0:T(128)S(1)}, s32[4]{0:T(128)}, u32[]{:S(2)}) copy-start(s32[4]{0:T(128)} %param.17) | copy-start | bytes 52
  7.2 174.3 %all-gather.3.cloned.1.call-start = ((), (), s32[]{:S(2)}) async-start(), calls=%async_computation | async-start | bytes 8650752 | tf_op jit(solution)/shard_map/all_gather | solution.py:85
  12.1 1.3 copy-start.2
  16.1 17.6 %copy-start.9 = (f32[4,2,128]{2,1,0:T(2,128)S(1)}, f32[4,2,128]{2,1,0:T(2,128)}, u32[]{:S(2)}) copy-start(f32[4,2,128]{2,1,0:T(2,128)} %param.15) | copy-start | bytes 12292
  26.9 327.5 %all-gather.5.cloned.1.call-start = ((), (), s32[]{:S(2)}) async-start(), calls=%async_computation.1 | async-start | bytes 8650752 | tf_op jit(solution)/shard_map/all_gather | solution.py:86
  28.0 4.7 collective-permute-start
  33.5 429.0 %all-reduce.2.cloned.1.call-start = ((), (), s32[]{:S(2)}) async-start(), calls=%async_computation.2 | async-start | bytes 2097152 | tf_op jit(solution)/shard_map/psum | solution.py:138
  35.3 1.0 copy-start.3
  35.3 1.0 copy-start.5
  36.3 149.2 %copy-start.8 = (s32[4352]{0:T(1024)S(1)}, s32[4352]{0:T(1024)}, u32[]{:S(2)}) copy-start(s32[4352]{0:T(1024)} %get-tuple-element.24) | copy-start | bytes 52228
  36.4 149.1 %copy-start.6 = (s32[4352]{0:T(1024)S(1)}, s32[4352]{0:T(1024)}, u32[]{:S(2)}) copy-start(s32[4352]{0:T(1024)} %copy-done.5) | copy-start | bytes 52228
  181.5 4.0 slice-start.2
  181.5 4.0 slice-start.3
  194.5 159.8 %copy-start.4 = (s32[4352]{0:T(1024)S(1)}, s32[4352]{0:T(1024)}, u32[]{:S(2)}) copy-start(s32[4352]{0:T(1024)} %copy-done.3) | copy-start | bytes 52228
  194.5 159.8 %copy-start.7 = (s32[4352]{0:T(1024)S(1)}, s32[4352]{0:T(1024)}, u32[]{:S(2)}) copy-start(s32[4352]{0:T(1024)} %get-tuple-element.23) | copy-start | bytes 52228
  354.4 4.0 slice-start
  354.4 4.0 slice-start.1
  361.0 5.5 %copy-start.12 = (f32[512,256]{1,0:T(8,128)S(1)}, f32[512,256]{1,0:T(8,128)}, u32[]{:S(2)}) copy-start(f32[512,256]{1,0:T(8,128)} %fusion.12) | copy-start | bytes 1572868
  366.4 3.2 copy-start.11
  369.6 92.8 %copy-start.1 = (bf16[256,2048]{1,0:T(8,128)(2,1)S(1)}, bf16[256,2048]{1,0:T(8,128)(2,1)}, u32[]{:S(2)}) copy-start(bf16[256,2048]{1,0:T(8,128)(2,1)} %param.9) | copy-start | bytes 3145732
  372.4 20.5 %collective-permute-start.1 = (bf16[256,256]{1,0:T(8,128)(2,1)S(1)}, bf16[256,256]{1,0:T(8,128)(2,1)S(1)}, u32[]{:S(2)}, u32[]{:S(2)}) collective-permute-start(bf16[256,256]{1,0:T(8,128)(2,1)S(1)} %get-tuple-element.38), channel_id=1, source_target_pairs={{0,4},{4,0},{1,5},{5,1},{2,6},{6,2},{3,7},{7,3},{8,12},{12,8},{9,1... | collective-permute-start | bytes 393224 | tf_op jit(solution)/shard_map/ppermute | solution.py:39
Sparse Core Ops, SparseCore 0:
  27.0 154.4 all-gather.2
  183.9 170.4 all-gather.4
  394.7 67.6 all-reduce.1
